TPU v7x, 512 devices: a whole 4x8x8 slice. The times are simulated.
512 devices in a mesh: chain: 64 (over y, z), sector: 8 (over x, core).
Axes of the slice: x: 4, y: 8, z: 8, core: 2. Of those that a mesh axis runs over, the one named last changes fastest.
Arguments:
- psi_start: bfloat16 [64, 16, 128, 128], P('chain', 'sector'), may hold values from -6 to 6
- left_terms: bfloat16 [64, 2, 16, 128, 128], P('chain', None, 'sector'), may hold values from -0.5 to 0.5
- left_rate: float32 [64, 2, 16, 128], P('chain', None, 'sector'), may hold values from 0.004 to 0.5
- right_terms: bfloat16 [64, 2, 16, 128, 128], P('chain', None, 'sector'), may hold values from -0.5 to 0.5
- right_rate: float32 [64, 2, 16, 128], P('chain', None, 'sector'), may hold values from 0.004 to 0.5
- term_left: int32 [12], replicated, may hold values from 0 to 1
- term_right: int32 [12], replicated, may hold values from 0 to 1
- term_shift: int32 [12], replicated, may hold values from -2 to 2
- term_coef: float32 [12], replicated, may hold values from 0.5 to 1.5
Outputs:
- psi_final: float32 [64, 16, 128, 128], P('chain', 'sector')
- rayleigh_cos: float32 [64], P('chain')
All inputs are finite; a program needn't handle non-finite values.
Results may differ from a plain program's by a relative error of at most 0.0058.
Values may be sent and summed in bfloat16 or wider, within the bound.
No kernel may reach another device: no remote copies, remote signals or barrier semaphores. Data moves between devices by JAX's collectives and lax.ppermute only.
A program may use at most 128 MiB of HBM per device.

v0:
```python
import jax
import jax.numpy as jnp
from jax import lax
from jax.sharding import PartitionSpec as P

ITERS = 4


epsilon = 1e-06


def carried_in(part, axis, combine, identity, reverse):
    count = lax.axis_size(axis)
    place = lax.axis_index(axis)
    ahead = count - 1 - place if reverse else place
    gathered = jax.tree.map(lambda a: lax.all_gather(a, axis), part)
    state = jax.tree.map(lambda a, e: jnp.zeros_like(a) + jnp.asarray(e, a.dtype), part, identity)

    def one(step, state):
        source = count - 1 - step if reverse else step
        return combine(
            state, jax.tree.map(lambda a: lax.dynamic_index_in_dim(a, source, 0, False), gathered)
        )

    return lax.fori_loop(0, ahead, one, state)


def with_halo(array, sides, width):
    for axis, dim in sides:
        peers, length = (lax.axis_size(axis), array.shape[dim])
        up = [(i, (i + 1) % peers) for i in range(peers - 1)]
        down = [(j, i) for i, j in up]
        last = lax.slice_in_dim(array, length - width, length, axis=dim)
        first = lax.slice_in_dim(array, 0, width, axis=dim)
        before = lax.ppermute(last, axis, up)
        after = lax.ppermute(first, axis, down)
        array = jnp.concatenate([before, array, after], axis=dim)
    return array


def combine_links(earlier, later):
    return (earlier[0] * later[0], later[0][..., None] * earlier[1] + later[1])


def body(
    psi_start,
    left_terms,
    left_rate,
    right_terms,
    right_rate,
    term_left,
    term_right,
    term_shift,
    term_coef,
):
    left_decay = jnp.exp(-left_rate[0])
    left_source = left_terms[0].astype(jnp.float32)
    left_prior = carried_in(
        (left_decay, left_source),
        "chain",
        combine_links,
        (jnp.ones_like(left_decay), jnp.zeros_like(left_source)),
        False,
    )
    left_env = (left_decay[..., None] * left_prior[1] + left_source).astype(jnp.bfloat16)
    right_decay = jnp.exp(-right_rate[0])
    right_source = right_terms[0].astype(jnp.float32)
    right_prior = carried_in(
        (right_decay, right_source),
        "chain",
        combine_links,
        (jnp.ones_like(right_decay), jnp.zeros_like(right_source)),
        True,
    )
    right_env = (right_decay[..., None] * right_prior[1] + right_source).astype(jnp.bfloat16)
    vector = psi_start[0].astype(jnp.float32)
    local_sectors = vector.shape[0]
    entries = vector.size * lax.axis_size("sector")
    cosine = jnp.zeros((), jnp.float32)
    for iteration in range(ITERS):
        rounded = vector.astype(jnp.bfloat16)
        padded = with_halo(rounded, (("sector", 0),), 2)

        def add_term(term_index, running):
            moved_block = lax.dynamic_slice_in_dim(
                padded, term_shift[term_index] + 2, local_sectors, 0
            )
            left_sel = lax.dynamic_index_in_dim(left_env, term_left[term_index], 0, keepdims=False)
            right_sel = lax.dynamic_index_in_dim(
                right_env, term_right[term_index], 0, keepdims=False
            )
            left_product = jnp.einsum(
                "sim,smj->sij", left_sel, moved_block, preferred_element_type=jnp.float32
            ).astype(jnp.bfloat16)
            full_product = jnp.einsum(
                "sim,sjm->sij", left_product, right_sel, preferred_element_type=jnp.float32
            )
            return running + term_coef[term_index] * full_product

        image = lax.fori_loop(0, term_coef.shape[0], add_term, jnp.zeros(vector.shape, jnp.float32))
        self_dot, cross_dot, image_dot = lax.psum(
            (jnp.sum(vector * vector), jnp.sum(vector * image), jnp.sum(image * image)), "sector"
        )
        rayleigh_now = cross_dot / self_dot
        step_size = 0.5 * jnp.sqrt(self_dot / (image_dot + epsilon))
        update = vector - step_size * (image - rayleigh_now * vector)
        update_sq = lax.psum(jnp.sum(update * update), "sector")
        vector = update * lax.rsqrt(update_sq / entries + epsilon)
        cosine = cross_dot * lax.rsqrt(self_dot * (image_dot + epsilon))
    return (vector[None], jnp.reshape(cosine, (1,)))


def solution(mesh):
    placed = (
        P("chain", "sector", None, None),
        P("chain", None, "sector", None, None),
        P("chain", None, "sector", None),
        P("chain", None, "sector", None, None),
        P("chain", None, "sector", None),
        P(),
        P(),
        P(),
        P(),
    )
    return jax.shard_map(
        body,
        mesh=mesh,
        in_specs=placed,
        out_specs=(P("chain", "sector", None, None), P("chain")),
        check_vma=False,
    )
```

profile of v0, /device:TPU:505, one launch (start us, length us, event | category | flops | bytes accessed | tf_op | source)
XLA Modules:
  0.0 1056.4 jit_solution(6927103977830681509)
XLA Ops:
  7.2 1.6 convert_element_type.82
  8.9 1.6 convert_element_type.78
  10.5 3.7 collective-permute-start
  14.2 1.9 collective-permute-start.1
  17.6 37.5 %all_gather.18 = f32[64,2,2,128]{3,2,1,0:T(2,128)S(1)} all-gather(f32[1,2,2,128]{3,2,1,0:T(2,128)S(1)} %get-tuple-element.1259), channel_id=1, replica_groups=mesh['chain'=64,'sector'=8] {'chain'}, dimensions={0}, use_global_device_ids=true | all-gather | bytes 133120 | tf_op jit(solution)/shard_map/all_gather | solution.py:16
  55.0 39.9 %all_gather.16 = f32[64,2,2,128]{3,2,1,0:T(2,128)S(1)} all-gather(f32[1,2,2,128]{3,2,1,0:T(2,128)S(1)} %get-tuple-element.1261), channel_id=1, replica_groups=mesh['chain'=64,'sector'=8] {'chain'}, dimensions={0}, use_global_device_ids=true | all-gather | bytes 133120 | tf_op jit(solution)/shard_map/all_gather | solution.py:16
  95.8 52.4 %all-gather.5.cloned.1.call-done = f32[64,2,2,128,128]{4,3,2,1,0:T(8,128)} async-done(((f32[1,2,2,128,128]{4,3,2,1,0:T(8,128)}), f32[64,2,2,128,128]{4,3,2,1,0:T(8,128)}) %all-gather.5.cloned.1.call-update) | async-done | bytes 16777232 | tf_op jit(solution)/shard_map/all_gather | solution.py:16
  148.2 141.1 %all-gather.3.cloned.1.call-done = f32[64,2,2,128,128]{4,3,2,1,0:T(8,128)} async-done(((f32[1,2,2,128,128]{4,3,2,1,0:T(8,128)}), f32[64,2,2,128,128]{4,3,2,1,0:T(8,128)}) %all-gather.3.cloned.1.call-update) | async-done | bytes 16777232 | tf_op jit(solution)/shard_map/all_gather | solution.py:16
  289.4 73.2 %while.90 = (s32[]{:T(128)}, f32[2,2,128,128]{3,2,1,0:T(8,128)S(1)}, s32[]{:T(128)}, f32[64,2,2,128]{3,2,1,0:T(2,128)S(1)}, f32[64,2,2,128,128]{4,3,2,1,0:T(8,128)}, /*index=5*/s32[]{:T(128)}, s32[]{:T(128)}, s32[]{:T(128)}) while((s32[]{:T(128)}, f32[2,2,128,128]{3,2,1,0:T(8,128)S(1)}, s32[]{:T(128)}, f32[64,2,2,128]{3,2,1,0:T(2,128)S(1)}, ...), condition=%wide.region_3.4_spmd, body=%wide.region_2.3_spmd.sunk | while | flops 131077 | bytes 792703 | solution.py:25
  363.8 133.5 %while.92 = (s32[]{:T(128)}, f32[2,128,128]{2,1,0:T(8,128)S(1)}, f32[12]{0:T(128)}, s32[12]{0:T(128)}, bf16[2,2,128,128]{3,2,1,0:T(8,128)(2,1)S(1)}, /*index=5*/...) while((s32[]{:T(128)}, f32[2,128,128]{2,1,0:T(8,128)S(1)}, ...), condition=%wide.region_7.8_spmd.clone, body=%wide.region_6.7_spmd.clone.sunk | while | flops 16908300 | bytes 459073 | solution.py:100
  497.3 1.6 multiply_reduce_fusion.13
  498.8 13.1 %all-reduce.3 = (f32[]{:T(128)}, f32[]{:T(128)}, f32[]{:T(128)}) all-reduce(f32[]{:T(128)} %get-tuple-element.1146, f32[]{:T(128)} %get-tuple-element.1147, f32[]{:T(128)} %get-tuple-element.1145), channel_id=1, replica_groups=mesh['chain'=64,'sector'=8] {'sector'}, use_global_device_ids=true, to_apply=%region_11.12 | all-reduce | flops 3 | bytes 24 | tf_op jit(solution)/shard_map/psum | solution.py:101
  514.4 1.5 multiply_reduce_fusion.12
  515.9 15.2 %psum.115 = f32[]{:T(128)} all-reduce(f32[]{:T(128)} %get-tuple-element.1256), channel_id=1, replica_groups=mesh['chain'=64,'sector'=8] {'sector'}, use_global_device_ids=true, to_apply=%region_13.14 | all-reduce | flops 1 | bytes 8 | tf_op jit(solution)/shard_map/psum | solution.py:107
  531.8 1.9 collective-permute-start.2
  533.7 2.4 collective-permute-start.3
  536.1 3.2 collective-permute-done.3
  539.3 133.5 %while.93 = (s32[]{:T(128)}, f32[2,128,128]{2,1,0:T(8,128)S(1)}, f32[12]{0:T(128)}, s32[12]{0:T(128)}, bf16[2,2,128,128]{3,2,1,0:T(8,128)(2,1)S(1)}, /*index=5*/...) while((s32[]{:T(128)}, f32[2,128,128]{2,1,0:T(8,128)S(1)}, ...), condition=%wide.region_17.18_spmd.clone, body=%wide.region_16.17_spmd.clone.sunk | while | flops 16908300 | bytes 459073 | solution.py:100
  673.5 10.5 all-reduce.2
  687.1 15.5 %psum.119 = f32[]{:T(128)} all-reduce(f32[]{:T(128)} %get-tuple-element.1254), channel_id=1, replica_groups=mesh['chain'=64,'sector'=8] {'sector'}, use_global_device_ids=true, to_apply=%region_23.24 | all-reduce | flops 1 | bytes 8 | tf_op jit(solution)/shard_map/psum | solution.py:107
  703.3 1.9 collective-permute-start.4
  705.3 2.4 collective-permute-start.5
  707.7 3.2 collective-permute-done.5
  710.9 133.5 %while.94 = (s32[]{:T(128)}, f32[2,128,128]{2,1,0:T(8,128)S(1)}, f32[12]{0:T(128)}, s32[12]{0:T(128)}, bf16[2,2,128,128]{3,2,1,0:T(8,128)(2,1)S(1)}, /*index=5*/...) while((s32[]{:T(128)}, f32[2,128,128]{2,1,0:T(8,128)S(1)}, ...), condition=%wide.region_27.28_spmd.clone, body=%wide.region_26.27_spmd.clone.sunk | while | flops 16908300 | bytes 459073 | solution.py:100
  845.1 10.5 all-reduce.1
  858.7 15.5 %psum.123 = f32[]{:T(128)} all-reduce(f32[]{:T(128)} %get-tuple-element.1252), channel_id=1, replica_groups=mesh['chain'=64,'sector'=8] {'sector'}, use_global_device_ids=true, to_apply=%region_33.34 | all-reduce | flops 1 | bytes 8 | tf_op jit(solution)/shard_map/psum | solution.py:107
  874.9 1.9 collective-permute-start.6
  876.9 2.4 collective-permute-start.7
  879.3 3.2 collective-permute-done.7
  882.5 133.5 %while.95 = (s32[]{:T(128)}, f32[2,128,128]{2,1,0:T(8,128)S(1)}, f32[12]{0:T(128)}, s32[12]{0:T(128)}, bf16[2,2,128,128]{3,2,1,0:T(8,128)(2,1)S(1)}, /*index=5*/...) while((s32[]{:T(128)}, f32[2,128,128]{2,1,0:T(8,128)S(1)}, ...), condition=%wide.region_37.38_spmd.clone, body=%wide.region_36.37_spmd.clone.sunk | while | flops 16908300 | bytes 459073 | solution.py:100
  1016.7 10.5 all-reduce
  1031.7 15.4 %psum.127 = f32[]{:T(128)} all-reduce(f32[]{:T(128)} %multiply_reduce_fusion), channel_id=1, replica_groups=mesh['chain'=64,'sector'=8] {'sector'}, use_global_device_ids=true, to_apply=%region_43.44 | all-reduce | flops 1 | bytes 8 | tf_op jit(solution)/shard_map/psum | solution.py:107
  (399 shorter events, 363.0 us)
Async XLA Ops:
  7.2 141.0 %all-gather.5.cloned.1.call-start = ((), (), s32[]{:S(2)}) async-start(), calls=%async_computation.1 | async-start | bytes 17039360 | tf_op jit(solution)/shard_map/all_gather | solution.py:16
  8.9 280.5 %all-gather.3.cloned.1.call-start = ((), (), s32[]{:S(2)}) async-start(), calls=%async_computation | async-start | bytes 17039360 | tf_op jit(solution)/shard_map/all_gather | solution.py:16
  10.5 84.4 %collective-permute-start = (bf16[2,128,128]{2,1,0:T(8,128)(2,1)}, bf16[2,128,128]{2,1,0:T(8,128)(2,1)S(1)}, u32[]{:S(2)}, u32[]{:S(2)}) collective-permute-start(bf16[2,128,128]{2,1,0:T(8,128)(2,1)} %bitcast.140), channel_id=1, source_target_pairs={{0,1},{1,2},{2,3},{3,4},{4,5},{5,6},{6,7},{8,9},{9,10},{10,11},{11... | collective-permute-start | bytes 196616 | tf_op jit(solution)/shard_map/ppermute | solution.py:35
  14.2 80.7 %collective-permute-start.1 = (bf16[2,128,128]{2,1,0:T(8,128)(2,1)}, bf16[2,128,128]{2,1,0:T(8,128)(2,1)S(1)}, u32[]{:S(2)}, u32[]{:S(2)}) collective-permute-start(bf16[2,128,128]{2,1,0:T(8,128)(2,1)} %bitcast.141), channel_id=1, source_target_pairs={{1,0},{2,1},{3,2},{4,3},{5,4},{6,5},{7,6},{9,8},{10,9},{11,10},{12... | collective-permute-start | bytes 196616 | tf_op jit(solution)/shard_map/ppermute | solution.py:36
  531.8 4.4 collective-permute-start.2
  533.7 5.6 collective-permute-start.3
  703.3 4.4 collective-permute-start.4
  705.3 5.6 collective-permute-start.5
  874.9 4.4 collective-permute-start.6
  876.9 5.6 collective-permute-start.7
Sparse Core Ops, SparseCore 0:
  11.0 137.1 all-gather.4
  151.2 138.1 all-gather.2
where the time goes:
time: 1070 us; the launch traced here: 1060 us
  loops' own time  253 us (24%)
  local copies, waits for them, and re-layouts  239 us (22%)
  waiting for transfers between devices  203 us (19%)
  blocking collectives  183 us (17%)
  other arithmetic  84.9 us (8%)
  matrix products  45 us (4%)
  between operations  29.4 us (3%)
  starting transfers between devices  18.7 us (2%)
    another operation x4, loops' own time, body(): lax.fori_loop(0, term_coef.shape[0], add_term, jnp.zeros(vector.shape, jn...  250 us
    all_gather x2, waiting for transfers between devices, carried_in(): gathered = jax.tree.map(lambda a: lax.all_gather(a, axis), part)  194 us
    all_gather x2, blocking collectives, carried_in(): gathered = jax.tree.map(lambda a: lax.all_gather(a, axis), part)  77.4 us
    add x63, other arithmetic, combine_links(): return (earlier[0] * later[0], later[0][..., None] * earlier[1] + later[1])  70.2 us
    psum x4, blocking collectives, body(): update_sq = lax.psum(jnp.sum(update * update), 'sector')  61.5 us
    dynamic_slice x48, local copies, waits for them, and re-layouts, add_term(): return running + term_coef[term_index] * full_product  59.7 us
    dynamic_slice x48, local copies, waits for them, and re-layouts, add_term(): term_left[term_index]  59.7 us
    dynamic_slice x48, local copies, waits for them, and re-layouts, add_term(): term_right[term_index]  59.7 us
  transfers between devices with their start and end apart: 10, of which 5 were waited for; matrix products, arithmetic and copies ran while one was open for 0% of the time, Pallas kernels for 0%

commit v1 on v0

v1 whole, which is shorter than its diff:
```python
import jax
import jax.numpy as jnp
from jax import lax
from jax.sharding import PartitionSpec as P

ITERS = 4
HALO = 2

epsilon = 1e-06


def chain_scan(decay, source, axis, reverse):
    count = lax.axis_size(axis)
    gain, total = decay, source
    distance = 1
    while distance < count:
        if reverse:
            pairs = [(i, i - distance) for i in range(distance, count)]
        else:
            pairs = [(i, i + distance) for i in range(count - distance)]
        got_gain, got_total = lax.ppermute((gain, total), axis, pairs)
        total = gain[..., None] * got_total + total
        if distance * 2 < count:
            gain = gain * got_gain
        distance *= 2
    return total


def body(
    psi_start,
    left_terms,
    left_rate,
    right_terms,
    right_rate,
    term_left,
    term_right,
    term_shift,
    term_coef,
):
    with jax.named_scope("psi_gather"):
        vector = lax.all_gather(psi_start[0], "sector", axis=0, tiled=True).astype(jnp.float32)
    with jax.named_scope("env_scan"):
        left_env = chain_scan(
            jnp.exp(-left_rate[0]), left_terms[0].astype(jnp.float32), "chain", False
        ).astype(jnp.bfloat16)
        right_env = chain_scan(
            jnp.exp(-right_rate[0]), right_terms[0].astype(jnp.float32), "chain", True
        ).astype(jnp.bfloat16)
    with jax.named_scope("env_gather"):
        left_env, right_env = lax.all_gather((left_env, right_env), "sector", axis=1, tiled=True)

    envs = left_env.shape[0]
    sectors = vector.shape[0]
    shifts = 2 * HALO + 1
    with jax.named_scope("term_table"):
        pick_right = (term_right[:, None] == jnp.arange(envs)[None]).astype(jnp.float32)
        pick_left = (term_left[:, None] == jnp.arange(envs)[None]).astype(jnp.float32)
        pick_shift = (term_shift[:, None] == jnp.arange(-HALO, HALO + 1)[None]).astype(jnp.float32)
        table = jnp.sum(
            term_coef[:, None, None, None]
            * pick_right[:, :, None, None]
            * pick_left[:, None, :, None]
            * pick_shift[:, None, None, :],
            axis=0,
        )

    entries = vector.size
    cosine = jnp.zeros((), jnp.float32)
    for iteration in range(ITERS):
        with jax.named_scope("apply_terms"):
            rounded = vector.astype(jnp.bfloat16)
            rim = jnp.zeros((HALO,) + rounded.shape[1:], jnp.bfloat16)
            padded = jnp.concatenate([rim, rounded, rim], axis=0)
            moved = jnp.stack([padded[t : t + sectors] for t in range(shifts)], axis=0)
            left_products = jnp.einsum(
                "esim,tsmj->etsij", left_env, moved, preferred_element_type=jnp.float32
            ).astype(jnp.bfloat16)
            summed = jnp.sum(
                table[:, :, :, None, None, None] * left_products[None].astype(jnp.float32),
                axis=(1, 2),
            )
            high = summed.astype(jnp.bfloat16)
            low = (summed - high.astype(jnp.float32)).astype(jnp.bfloat16)
            image = jnp.einsum(
                "rsim,rsjm->sij", high, right_env, preferred_element_type=jnp.float32
            ) + jnp.einsum("rsim,rsjm->sij", low, right_env, preferred_element_type=jnp.float32)
        with jax.named_scope("residual_step"):
            self_dot = jnp.sum(vector * vector)
            cross_dot = jnp.sum(vector * image)
            image_dot = jnp.sum(image * image)
            rayleigh_now = cross_dot / self_dot
            step_size = 0.5 * jnp.sqrt(self_dot / (image_dot + epsilon))
            update = vector - step_size * (image - rayleigh_now * vector)
            vector = update * lax.rsqrt(jnp.sum(update * update) / entries + epsilon)
            cosine = cross_dot * lax.rsqrt(self_dot * (image_dot + epsilon))
    local = psi_start.shape[1]
    mine = lax.dynamic_slice_in_dim(vector, lax.axis_index("sector") * local, local, 0)
    return (mine[None], jnp.reshape(cosine, (1,)))


def solution(mesh):
    placed = (
        P("chain", "sector", None, None),
        P("chain", None, "sector", None, None),
        P("chain", None, "sector", None),
        P("chain", None, "sector", None, None),
        P("chain", None, "sector", None),
        P(),
        P(),
        P(),
        P(),
    )
    return jax.shard_map(
        body,
        mesh=mesh,
        in_specs=placed,
        out_specs=(P("chain", "sector", None, None), P("chain")),
        check_vma=False,
    )
```

time: 1070 us -> 321 us (0.30)
  the two profiles are of different devices: /device:TPU:505 before, /device:TPU:1 now
where the time goes in v1:
time: 321 us; the launch traced here: 315 us
  starting transfers between devices  90.4 us (28%)
  local copies, waits for them, and re-layouts  54.9 us (17%)
  other arithmetic  43.5 us (14%)
  matrix products  43 us (13%)
  waiting for transfers between devices  34.3 us (11%)
  between operations  31.2 us (10%)
  blocking collectives  17.9 us (6%)
    ppermute x22, starting transfers between devices, chain_scan(): got_gain, got_total = lax.ppermute((gain, total), axis, pairs)  90.3 us
    convert_element_type x4, local copies, waits for them, and re-layouts, body(): left_products[None].astype(jnp.float32)  45.2 us
    ppermute x22, waiting for transfers between devices, chain_scan(): got_gain, got_total = lax.ppermute((gain, total), axis, pairs)  31 us
    reduce_sum x4, other arithmetic, body(): jnp.sum(table[:, :, :, None, None, None] * left_products[None].astype(jnp...  28.1 us
    dot_general x4, matrix products, body(): jnp.einsum('esim,tsmj->etsij', left_env, moved, preferred_element_type=jn...  23.6 us
    all_gather x1, blocking collectives, body(): lax.all_gather(psi_start[0], 'sector', axis=0, tiled=True)  17.9 us
    dot_general x4, matrix products, body(): jnp.einsum('rsim,rsjm->sij', low, right_env, preferred_element_type=jnp.f...  11.6 us
    dot_general x4, matrix products, body(): jnp.einsum('rsim,rsjm->sij', high, right_env, preferred_element_type=jnp....  7.8 us
  transfers between devices with their start and end apart: 24, of which 9 were waited for; matrix products, arithmetic and copies ran while one was open for 12% of the time, Pallas kernels for 0%

profile of v1, /device:TPU:1, one launch (start us, length us, event | category | flops | bytes accessed | tf_op | source)
XLA Modules:
  0.0 315.1 jit_solution(15505031694861749103)
XLA Ops:
  8.2 4.8 %collective-permute-start.5 = (f32[2,2,128,128]{3,2,0,1:T(8,128)S(1)}, f32[2,2,128,128]{3,2,0,1:T(8,128)S(1)}, u32[]{:S(2)}, u32[]{:S(2)}) collective-permute-start(f32[2,2,128,128]{3,2,0,1:T(8,128)S(1)} %bitcast_convert_fusion.1), channel_id=1, source_target_pairs={{0,8},{8,16},{16,24},{24,32},{32,40},{40,48},{48,56},{56,64},{64,7... | collective-permute-start | bytes 786440 | tf_op jit(solution)/shard_map/env_scan/ppermute | solution.py:21
  17.3 7.7 %collective-permute-start.6 = (f32[2,2,128,128]{3,2,0,1:T(8,128)S(1)}, f32[2,2,128,128]{3,2,0,1:T(8,128)S(1)}, u32[]{:S(2)}, u32[]{:S(2)}) collective-permute-start(f32[2,2,128,128]{3,2,0,1:T(8,128)S(1)} %multiply_add_fusion.9), channel_id=1, source_target_pairs={{0,16},{8,24},{16,32},{24,40},{32,48},{40,56},{48,64},{56,72},{64,... | collective-permute-start | bytes 786440 | tf_op jit(solution)/shard_map/env_scan/ppermute | solution.py:21
  25.1 5.1 %collective-permute-start = (f32[2,2,128]{2,1,0:T(2,128)S(1)}, f32[2,2,128]{2,1,0:T(2,128)S(1)}, u32[]{:S(2)}, u32[]{:S(2)}) collective-permute-start(f32[2,2,128]{2,1,0:T(2,128)S(1)} %exponential_bitcast_fusion.1), channel_id=1, source_target_pairs={{0,8},{8,16},{16,24},{24,32},{32,40},{40,48},{48,56},{56,64},{64,7... | collective-permute-start | bytes 6152 | tf_op jit(solution)/shard_map/env_scan/ppermute | solution.py:21
  31.7 15.8 %collective-permute-start.7 = (f32[2,2,128,128]{3,2,0,1:T(8,128)S(1)}, f32[2,2,128,128]{3,2,0,1:T(8,128)S(1)}, u32[]{:S(2)}, u32[]{:S(2)}) collective-permute-start(f32[2,2,128,128]{3,2,0,1:T(8,128)S(1)} %multiply_add_fusion.8), channel_id=1, source_target_pairs={{0,32},{8,40},{16,48},{24,56},{32,64},{40,72},{48,80},{56,88},{64,... | collective-permute-start | bytes 786440 | tf_op jit(solution)/shard_map/env_scan/ppermute | solution.py:21
  51.7 11.2 %collective-permute-start.2 = (f32[2,2,128]{2,1,0:T(2,128)S(1)}, f32[2,2,128]{2,1,0:T(2,128)S(1)}, u32[]{:S(2)}, u32[]{:S(2)}) collective-permute-start(f32[2,2,128]{2,1,0:T(2,128)S(1)} %mul.365), channel_id=1, source_target_pairs={{0,32},{8,40},{16,48},{24,56},{32,64},{40,72},{48,80},{56,88},{64,... | collective-permute-start | bytes 6152 | tf_op jit(solution)/shard_map/env_scan/ppermute | solution.py:21
  63.0 4.4 %collective-permute-start.8 = (f32[2,2,128,128]{3,2,0,1:T(8,128)S(1)}, f32[2,2,128,128]{3,2,0,1:T(8,128)S(1)}, u32[]{:S(2)}, u32[]{:S(2)}) collective-permute-start(f32[2,2,128,128]{3,2,0,1:T(8,128)S(1)} %multiply_add_fusion.7), channel_id=1, source_target_pairs={{0,64},{8,72},{16,80},{24,88},{32,96},{40,104},{48,112},{56,120},{... | collective-permute-start | bytes 786440 | tf_op jit(solution)/shard_map/env_scan/ppermute | solution.py:21
  68.9 5.2 %collective-permute-start.3 = (f32[2,2,128]{2,1,0:T(2,128)S(1)}, f32[2,2,128]{2,1,0:T(2,128)S(1)}, u32[]{:S(2)}, u32[]{:S(2)}) collective-permute-start(f32[2,2,128]{2,1,0:T(2,128)S(1)} %mul.366), channel_id=1, source_target_pairs={{0,64},{8,72},{16,80},{24,88},{32,96},{40,104},{48,112},{56,120},{... | collective-permute-start | bytes 6152 | tf_op jit(solution)/shard_map/env_scan/ppermute | solution.py:21
  75.9 7.0 %collective-permute-start.9 = (f32[2,2,128,128]{3,2,0,1:T(8,128)S(1)}, f32[2,2,128,128]{3,2,0,1:T(8,128)S(1)}, u32[]{:S(2)}, u32[]{:S(2)}) collective-permute-start(f32[2,2,128,128]{3,2,0,1:T(8,128)S(1)} %multiply_add_fusion.6), channel_id=1, source_target_pairs={{0,128},{8,136},{16,144},{24,152},{32,160},{40,168},{48,176},{56,1... | collective-permute-start | bytes 786440 | tf_op jit(solution)/shard_map/env_scan/ppermute | solution.py:21
  84.3 5.6 %collective-permute-start.4 = (f32[2,2,128]{2,1,0:T(2,128)S(1)}, f32[2,2,128]{2,1,0:T(2,128)S(1)}, u32[]{:S(2)}, u32[]{:S(2)}) collective-permute-start(f32[2,2,128]{2,1,0:T(2,128)S(1)} %mul.367), channel_id=1, source_target_pairs={{0,128},{8,136},{16,144},{24,152},{32,160},{40,168},{48,176},{56,1... | collective-permute-start | bytes 6152 | tf_op jit(solution)/shard_map/env_scan/ppermute | solution.py:21
  92.9 7.1 %collective-permute-start.10 = (f32[2,2,128,128]{3,2,0,1:T(8,128)S(1)}, f32[2,2,128,128]{3,2,0,1:T(8,128)S(1)}, u32[]{:S(2)}, u32[]{:S(2)}) collective-permute-start(f32[2,2,128,128]{3,2,0,1:T(8,128)S(1)} %multiply_add_fusion.5), channel_id=1, source_target_pairs={{0,256},{8,264},{16,272},{24,280},{32,288},{40,296},{48,304},{56,3... | collective-permute-start | bytes 786440 | tf_op jit(solution)/shard_map/env_scan/ppermute | solution.py:21
  100.1 17.9 %all-gather = bf16[1,16,128,128]{3,2,0,1:T(8,128)(2,1)S(1)} all-gather(bf16[1,2,128,128]{3,2,0,1:T(8,128)(2,1)S(1)} %bitcast.167), channel_id=2, replica_groups=mesh['chain'=64,'sector'=8] {'sector'}, dimensions={1}, use_global_device_ids=true | all-gather | bytes 589824 | tf_op jit(solution)/shard_map/psi_gather/all_gather | solution.py:41
  121.7 6.9 %collective-permute-done.13 = f32[2,2,128]{2,1,0:T(2,128)S(1)} collective-permute-done((f32[2,2,128]{2,1,0:T(2,128)S(1)}, f32[2,2,128]{2,1,0:T(2,128)S(1)}, u32[]{:S(2)}, u32[]{:S(2)}) %collective-permute-start.13) | collective-permute-done | bytes 2080 | tf_op jit(solution)/shard_map/env_scan/ppermute | solution.py:21
  131.4 4.2 %collective-permute-done.14 = f32[2,2,128]{2,1,0:T(2,128)S(1)} collective-permute-done((f32[2,2,128]{2,1,0:T(2,128)S(1)}, f32[2,2,128]{2,1,0:T(2,128)S(1)}, u32[]{:S(2)}, u32[]{:S(2)}) %collective-permute-start.14) | collective-permute-done | bytes 2080 | tf_op jit(solution)/shard_map/env_scan/ppermute | solution.py:21
  135.6 7.1 %collective-permute-done.20 = f32[2,2,128,128]{3,2,0,1:T(8,128)S(1)} collective-permute-done((f32[2,2,128,128]{3,2,0,1:T(8,128)S(1)}, f32[2,2,128,128]{3,2,0,1:T(8,128)S(1)}, u32[]{:S(2)}, u32[]{:S(2)}) %collective-permute-start.20) | collective-permute-done | bytes 262176 | tf_op jit(solution)/shard_map/env_scan/ppermute | solution.py:21
  146.2 3.2 %collective-permute-done.15 = f32[2,2,128]{2,1,0:T(2,128)S(1)} collective-permute-done((f32[2,2,128]{2,1,0:T(2,128)S(1)}, f32[2,2,128]{2,1,0:T(2,128)S(1)}, u32[]{:S(2)}, u32[]{:S(2)}) %collective-permute-start.15) | collective-permute-done | bytes 2080 | tf_op jit(solution)/shard_map/env_scan/ppermute | solution.py:21
  149.4 4.9 %collective-permute-done.21 = f32[2,2,128,128]{3,2,0,1:T(8,128)S(1)} collective-permute-done((f32[2,2,128,128]{3,2,0,1:T(8,128)S(1)}, f32[2,2,128,128]{3,2,0,1:T(8,128)S(1)}, u32[]{:S(2)}, u32[]{:S(2)}) %collective-permute-start.21) | collective-permute-done | bytes 262176 | tf_op jit(solution)/shard_map/env_scan/ppermute | solution.py:21
  159.6 7.5 %convert_bitcast_fusion.3 = f32[2,5,16,128,128]{3,4,0,1,2:T(8,128)} fusion(bf16[5,16,128,128]{2,3,0,1:T(8,128)(2,1)} %fusion.23, bf16[2,16,128,128]{3,2,0,1:T(8,128)(2,1)} %all-gather.4.cloned.1.call-done), kind=kOutput, calls=%fused_computation.7 | convolution fusion | flops 676331520 | bytes 14155776 | tf_op jit(solution)/shard_map/apply_terms/esim,tsmj->etsij/dot_general | solution.py:75
  167.1 11.3 %copy.130 = f32[2,5,16,128,128]{4,3,2,1,0:T(8,128)} copy(f32[2,5,16,128,128]{3,4,0,1,2:T(8,128)} %convert_bitcast_fusion.3) | data formatting | bytes 20971520 | tf_op jit(solution)/shard_map/apply_terms/convert_element_type | solution.py:79
  178.4 7.2 %multiply_reduce_fusion.3 = f32[2,16,128,128]{3,2,1,0:T(8,128)} fusion(f32[2,5,16,128,128]{4,3,2,1,0:T(8,128)} %copy.130, f32[2,2,5]{2,1,0:T(2,128)S(1)} %copy.118), kind=kLoop, calls=%fused_computation.3 | loop fusion | flops 9961472 | bytes 12582992 | tf_op jit(solution)/shard_map/apply_terms/reduce_sum | solution.py:78
  185.6 3.3 %all-gather.6.cloned.1.call-done = bf16[2,16,128,128]{3,2,0,1:T(8,128)(2,1)} async-done(((bf16[2,2,128,128]{3,2,0,1:T(8,128)(2,1)}), bf16[2,16,128,128]{3,2,0,1:T(8,128)(2,1)}) %all-gather.6.cloned.1.call-update) | async-done | bytes 1048592 | tf_op jit(solution)/shard_map/env_gather/all_gather | solution.py:50
  188.9 3.1 convolution_bitcast_fusion.6
  201.5 5.4 %convert_bitcast_fusion.2 = f32[2,5,16,128,128]{3,4,0,1,2:T(8,128)} fusion(bf16[2,16,128,128]{3,2,0,1:T(8,128)(2,1)S(1)} %copy-done.5, bf16[5,16,128,128]{2,3,1,0:T(8,128)(2,1)S(1)} %fusion.31), kind=kOutput, calls=%fused_computation.6 | convolution fusion | flops 676331520 | bytes 14155776 | tf_op jit(solution)/shard_map/apply_terms/esim,tsmj->etsij/dot_general | solution.py:75
  206.9 11.3 %copy.143 = f32[2,5,16,128,128]{4,3,2,1,0:T(8,128)} copy(f32[2,5,16,128,128]{3,4,0,1,2:T(8,128)} %convert_bitcast_fusion.2) | data formatting | bytes 20971520 | tf_op jit(solution)/shard_map/apply_terms/convert_element_type | solution.py:79
  218.2 7.0 %multiply_reduce_fusion.2 = f32[2,16,128,128]{3,2,1,0:T(8,128)} fusion(f32[2,5,16,128,128]{4,3,2,1,0:T(8,128)} %copy.143, f32[2,2,5]{2,1,0:T(2,128)S(1)} %copy.118), kind=kLoop, calls=%fused_computation.2 | loop fusion | flops 9961472 | bytes 12582992 | tf_op jit(solution)/shard_map/apply_terms/reduce_sum | solution.py:78
  225.2 2.8 convolution_bitcast_fusion.4
  237.2 5.4 %convert_bitcast_fusion.1 = f32[2,5,16,128,128]{3,4,0,1,2:T(8,128)} fusion(bf16[2,16,128,128]{3,2,0,1:T(8,128)(2,1)S(1)} %copy-done.6, bf16[5,16,128,128]{2,3,1,0:T(8,128)(2,1)S(1)} %fusion.39), kind=kOutput, calls=%fused_computation.5 | convolution fusion | flops 676331520 | bytes 14155776 | tf_op jit(solution)/shard_map/apply_terms/esim,tsmj->etsij/dot_general | solution.py:75
  242.5 11.3 %copy.149 = f32[2,5,16,128,128]{4,3,2,1,0:T(8,128)} copy(f32[2,5,16,128,128]{3,4,0,1,2:T(8,128)} %convert_bitcast_fusion.1) | data formatting | bytes 20971520 | tf_op jit(solution)/shard_map/apply_terms/convert_element_type | solution.py:79
  253.9 7.0 %multiply_reduce_fusion.1 = f32[2,16,128,128]{3,2,1,0:T(8,128)} fusion(f32[2,5,16,128,128]{4,3,2,1,0:T(8,128)} %copy.149, f32[2,2,5]{2,1,0:T(2,128)S(1)} %copy.118), kind=kLoop, calls=%fused_computation.1 | loop fusion | flops 9961472 | bytes 12582992 | tf_op jit(solution)/shard_map/apply_terms/reduce_sum | solution.py:78
  260.8 2.8 convolution_bitcast_fusion.2
  272.9 5.4 %convert_bitcast_fusion = f32[2,5,16,128,128]{3,4,0,1,2:T(8,128)} fusion(bf16[2,16,128,128]{3,2,0,1:T(8,128)(2,1)S(1)} %copy-done.7, bf16[5,16,128,128]{2,3,1,0:T(8,128)(2,1)S(1)} %fusion.47), kind=kOutput, calls=%fused_computation.4 | convolution fusion | flops 676331520 | bytes 14155776 | tf_op jit(solution)/shard_map/apply_terms/esim,tsmj->etsij/dot_general | solution.py:75
  278.2 11.3 %copy.155 = f32[2,5,16,128,128]{4,3,2,1,0:T(8,128)} copy(f32[2,5,16,128,128]{3,4,0,1,2:T(8,128)} %convert_bitcast_fusion) | data formatting | bytes 20971520 | tf_op jit(solution)/shard_map/apply_terms/convert_element_type | solution.py:79
  289.5 7.0 %multiply_reduce_fusion = f32[2,16,128,128]{3,2,1,0:T(8,128)} fusion(f32[2,5,16,128,128]{4,3,2,1,0:T(8,128)} %copy.155, f32[2,2,5]{2,1,0:T(2,128)S(1)} %copy.118), kind=kLoop, calls=%fused_computation | loop fusion | flops 9961472 | bytes 12582992 | tf_op jit(solution)/shard_map/apply_terms/reduce_sum | solution.py:78
  (145 shorter events, 56.8 us)
Async XLA Ops:
  7.2 67.0 %copy-start.8 = (bf16[1,2,2,128,128]{4,3,2,1,0:T(8,128)(2,1)S(1)}, bf16[1,2,2,128,128]{4,3,2,1,0:T(8,128)(2,1)}, u32[]{:S(2)}) copy-start(bf16[1,2,2,128,128]{4,3,2,1,0:T(8,128)(2,1)} %param.12) | copy-start | bytes 393220
  7.2 60.3 %copy-start.10 = (f32[1,2,2,128]{3,2,1,0:T(2,128)S(1)}, f32[1,2,2,128]{3,2,1,0:T(2,128)}, u32[]{:S(2)}) copy-start(f32[1,2,2,128]{3,2,1,0:T(2,128)} %param.13) | copy-start | bytes 6148
  7.2 152.4 %all-gather.4.cloned.1.call-start = ((), (), s32[]{:S(2)}) async-start(), calls=%async_computation | async-start | bytes 1179648 | tf_op jit(solution)/shard_map/env_gather/all_gather | solution.py:50
  8.2 8.1 %collective-permute-start.5 = (f32[2,2,128,128]{3,2,0,1:T(8,128)S(1)}, f32[2,2,128,128]{3,2,0,1:T(8,128)S(1)}, u32[]{:S(2)}, u32[]{:S(2)}) collective-permute-start(f32[2,2,128,128]{3,2,0,1:T(8,128)S(1)} %bitcast_convert_fusion.1), channel_id=1, source_target_pairs={{0,8},{8,16},{16,24},{24,32},{32,40},{40,48},{48,56},{56,64},{64,7... | collective-permute-start | bytes 786440 | tf_op jit(solution)/shard_map/env_scan/ppermute | solution.py:21
  17.3 82.7 %copy-start.9 = (bf16[1,2,128,128]{3,2,1,0:T(8,128)(2,1)S(1)}, bf16[1,2,128,128]{3,2,1,0:T(8,128)(2,1)}, u32[]{:S(2)}) copy-start(bf16[1,2,128,128]{3,2,1,0:T(8,128)(2,1)} %param.9) | copy-start | bytes 196612
  17.3 14.2 %collective-permute-start.6 = (f32[2,2,128,128]{3,2,0,1:T(8,128)S(1)}, f32[2,2,128,128]{3,2,0,1:T(8,128)S(1)}, u32[]{:S(2)}, u32[]{:S(2)}) collective-permute-start(f32[2,2,128,128]{3,2,0,1:T(8,128)S(1)} %multiply_add_fusion.9), channel_id=1, source_target_pairs={{0,16},{8,24},{16,32},{24,40},{32,48},{40,56},{48,64},{56,72},{64,... | collective-permute-start | bytes 786440 | tf_op jit(solution)/shard_map/env_scan/ppermute | solution.py:21
  25.1 5.8 %collective-permute-start = (f32[2,2,128]{2,1,0:T(2,128)S(1)}, f32[2,2,128]{2,1,0:T(2,128)S(1)}, u32[]{:S(2)}, u32[]{:S(2)}) collective-permute-start(f32[2,2,128]{2,1,0:T(2,128)S(1)} %exponential_bitcast_fusion.1), channel_id=1, source_target_pairs={{0,8},{8,16},{16,24},{24,32},{32,40},{40,48},{48,56},{56,64},{64,7... | collective-permute-start | bytes 6152 | tf_op jit(solution)/shard_map/env_scan/ppermute | solution.py:21
  31.7 31.2 %collective-permute-start.7 = (f32[2,2,128,128]{3,2,0,1:T(8,128)S(1)}, f32[2,2,128,128]{3,2,0,1:T(8,128)S(1)}, u32[]{:S(2)}, u32[]{:S(2)}) collective-permute-start(f32[2,2,128,128]{3,2,0,1:T(8,128)S(1)} %multiply_add_fusion.8), channel_id=1, source_target_pairs={{0,32},{8,40},{16,48},{24,56},{32,64},{40,72},{48,80},{56,88},{64,... | collective-permute-start | bytes 786440 | tf_op jit(solution)/shard_map/env_scan/ppermute | solution.py:21
  47.5 4.2 %collective-permute-start.1 = (f32[2,2,128]{2,1,0:T(2,128)S(1)}, f32[2,2,128]{2,1,0:T(2,128)S(1)}, u32[]{:S(2)}, u32[]{:S(2)}) collective-permute-start(f32[2,2,128]{2,1,0:T(2,128)S(1)} %fusion.64), channel_id=1, source_target_pairs={{0,16},{8,24},{16,32},{24,40},{32,48},{40,56},{48,64},{56,72},{64,... | collective-permute-start | bytes 6152 | tf_op jit(solution)/shard_map/env_scan/ppermute | solution.py:21
  50.4 23.7 %collective-permute-start.16 = (f32[2,2,128,128]{3,2,0,1:T(8,128)S(1)}, f32[2,2,128,128]{3,2,0,1:T(8,128)S(1)}, u32[]{:S(2)}, u32[]{:S(2)}) collective-permute-start(f32[2,2,128,128]{3,2,0,1:T(8,128)S(1)} %bitcast_convert_fusion), channel_id=1, source_target_pairs={{8,0},{16,8},{24,16},{32,24},{40,32},{48,40},{56,48},{64,56},{72,6... | collective-permute-start | bytes 786440 | tf_op jit(solution)/shard_map/env_scan/ppermute | solution.py:21
  51.7 17.1 %collective-permute-start.2 = (f32[2,2,128]{2,1,0:T(2,128)S(1)}, f32[2,2,128]{2,1,0:T(2,128)S(1)}, u32[]{:S(2)}, u32[]{:S(2)}) collective-permute-start(f32[2,2,128]{2,1,0:T(2,128)S(1)} %mul.365), channel_id=1, source_target_pairs={{0,32},{8,40},{16,48},{24,56},{32,64},{40,72},{48,80},{56,88},{64,... | collective-permute-start | bytes 6152 | tf_op jit(solution)/shard_map/env_scan/ppermute | solution.py:21
  63.0 12.7 %collective-permute-start.8 = (f32[2,2,128,128]{3,2,0,1:T(8,128)S(1)}, f32[2,2,128,128]{3,2,0,1:T(8,128)S(1)}, u32[]{:S(2)}, u32[]{:S(2)}) collective-permute-start(f32[2,2,128,128]{3,2,0,1:T(8,128)S(1)} %multiply_add_fusion.7), channel_id=1, source_target_pairs={{0,64},{8,72},{16,80},{24,88},{32,96},{40,104},{48,112},{56,120},{... | collective-permute-start | bytes 786440 | tf_op jit(solution)/shard_map/env_scan/ppermute | solution.py:21
  67.5 15.4 %collective-permute-start.11 = (f32[2,2,128]{2,1,0:T(2,128)S(1)}, f32[2,2,128]{2,1,0:T(2,128)S(1)}, u32[]{:S(2)}, u32[]{:S(2)}) collective-permute-start(f32[2,2,128]{2,1,0:T(2,128)S(1)} %exponential_bitcast_fusion), channel_id=1, source_target_pairs={{8,0},{16,8},{24,16},{32,24},{40,32},{48,40},{56,48},{64,56},{72,6... | collective-permute-start | bytes 6152 | tf_op jit(solution)/shard_map/env_scan/ppermute | solution.py:21
  68.9 52.8 %copy-start.11 = (s32[12]{0:T(128)S(1)}, s32[12]{0:T(128)}, u32[]{:S(2)}) copy-start(s32[12]{0:T(128)} %param.16) | copy-start | bytes 148
  68.9 15.3 %collective-permute-start.3 = (f32[2,2,128]{2,1,0:T(2,128)S(1)}, f32[2,2,128]{2,1,0:T(2,128)S(1)}, u32[]{:S(2)}, u32[]{:S(2)}) collective-permute-start(f32[2,2,128]{2,1,0:T(2,128)S(1)} %mul.366), channel_id=1, source_target_pairs={{0,64},{8,72},{16,80},{24,88},{32,96},{40,104},{48,112},{56,120},{... | collective-permute-start | bytes 6152 | tf_op jit(solution)/shard_map/env_scan/ppermute | solution.py:21
  74.3 55.7 %copy-start.12 = (f32[12]{0:T(128)S(1)}, f32[12]{0:T(128)}, u32[]{:S(2)}) copy-start(f32[12]{0:T(128)} %param.17) | copy-start | bytes 148
  74.3 55.7 %copy-start.13 = (s32[12]{0:T(128)S(1)}, s32[12]{0:T(128)}, u32[]{:S(2)}) copy-start(s32[12]{0:T(128)} %param.15) | copy-start | bytes 148
  74.3 57.0 %copy-start.14 = (s32[12]{0:T(128)S(1)}, s32[12]{0:T(128)}, u32[]{:S(2)}) copy-start(s32[12]{0:T(128)} %param.14) | copy-start | bytes 148
  74.3 17.0 %collective-permute-start.17 = (f32[2,2,128,128]{3,2,0,1:T(8,128)S(1)}, f32[2,2,128,128]{3,2,0,1:T(8,128)S(1)}, u32[]{:S(2)}, u32[]{:S(2)}) collective-permute-start(f32[2,2,128,128]{3,2,0,1:T(8,128)S(1)} %multiply_add_fusion.4), channel_id=1, source_target_pairs={{16,0},{24,8},{32,16},{40,24},{48,32},{56,40},{64,48},{72,56},{80,... | collective-permute-start | bytes 786440 | tf_op jit(solution)/shard_map/env_scan/ppermute | solution.py:21
  75.9 16.9 %collective-permute-start.9 = (f32[2,2,128,128]{3,2,0,1:T(8,128)S(1)}, f32[2,2,128,128]{3,2,0,1:T(8,128)S(1)}, u32[]{:S(2)}, u32[]{:S(2)}) collective-permute-start(f32[2,2,128,128]{3,2,0,1:T(8,128)S(1)} %multiply_add_fusion.6), channel_id=1, source_target_pairs={{0,128},{8,136},{16,144},{24,152},{32,160},{40,168},{48,176},{56,1... | collective-permute-start | bytes 786440 | tf_op jit(solution)/shard_map/env_scan/ppermute | solution.py:21
  82.9 35.0 %collective-permute-start.12 = (f32[2,2,128]{2,1,0:T(2,128)S(1)}, f32[2,2,128]{2,1,0:T(2,128)S(1)}, u32[]{:S(2)}, u32[]{:S(2)}) collective-permute-start(f32[2,2,128]{2,1,0:T(2,128)S(1)} %fusion.65), channel_id=1, source_target_pairs={{16,0},{24,8},{32,16},{40,24},{48,32},{56,40},{64,48},{72,56},{80,... | collective-permute-start | bytes 6152 | tf_op jit(solution)/shard_map/env_scan/ppermute | solution.py:21
  84.3 33.7 %collective-permute-start.4 = (f32[2,2,128]{2,1,0:T(2,128)S(1)}, f32[2,2,128]{2,1,0:T(2,128)S(1)}, u32[]{:S(2)}, u32[]{:S(2)}) collective-permute-start(f32[2,2,128]{2,1,0:T(2,128)S(1)} %mul.367), channel_id=1, source_target_pairs={{0,128},{8,136},{16,144},{24,152},{32,160},{40,168},{48,176},{56,1... | collective-permute-start | bytes 6152 | tf_op jit(solution)/shard_map/env_scan/ppermute | solution.py:21
  91.5 26.5 %collective-permute-start.18 = (f32[2,2,128,128]{3,2,0,1:T(8,128)S(1)}, f32[2,2,128,128]{3,2,0,1:T(8,128)S(1)}, u32[]{:S(2)}, u32[]{:S(2)}) collective-permute-start(f32[2,2,128,128]{3,2,0,1:T(8,128)S(1)} %multiply_add_fusion.3), channel_id=1, source_target_pairs={{32,0},{40,8},{48,16},{56,24},{64,32},{72,40},{80,48},{88,56},{96,... | collective-permute-start | bytes 786440 | tf_op jit(solution)/shard_map/env_scan/ppermute | solution.py:21
  92.9 26.5 %collective-permute-start.10 = (f32[2,2,128,128]{3,2,0,1:T(8,128)S(1)}, f32[2,2,128,128]{3,2,0,1:T(8,128)S(1)}, u32[]{:S(2)}, u32[]{:S(2)}) collective-permute-start(f32[2,2,128,128]{3,2,0,1:T(8,128)S(1)} %multiply_add_fusion.5), channel_id=1, source_target_pairs={{0,256},{8,264},{16,272},{24,280},{32,288},{40,296},{48,304},{56,3... | collective-permute-start | bytes 786440 | tf_op jit(solution)/shard_map/env_scan/ppermute | solution.py:21
  118.1 10.4 %collective-permute-start.19 = (f32[2,2,128,128]{3,2,0,1:T(8,128)S(1)}, f32[2,2,128,128]{3,2,0,1:T(8,128)S(1)}, u32[]{:S(2)}, u32[]{:S(2)}) collective-permute-start(f32[2,2,128,128]{3,2,0,1:T(8,128)S(1)} %multiply_add_fusion.2), channel_id=1, source_target_pairs={{64,0},{72,8},{80,16},{88,24},{96,32},{104,40},{112,48},{120,56},{... | collective-permute-start | bytes 786440 | tf_op jit(solution)/shard_map/env_scan/ppermute | solution.py:21
  120.3 68.6 %all-gather.6.cloned.1.call-start = ((), (), s32[]{:S(2)}) async-start(), calls=%async_computation.1 | async-start | bytes 1179648 | tf_op jit(solution)/shard_map/env_gather/all_gather | solution.py:50
  120.3 8.2 %collective-permute-start.13 = (f32[2,2,128]{2,1,0:T(2,128)S(1)}, f32[2,2,128]{2,1,0:T(2,128)S(1)}, u32[]{:S(2)}, u32[]{:S(2)}) collective-permute-start(f32[2,2,128]{2,1,0:T(2,128)S(1)} %mul.384), channel_id=1, source_target_pairs={{32,0},{40,8},{48,16},{56,24},{64,32},{72,40},{80,48},{88,56},{96,... | collective-permute-start | bytes 6152 | tf_op jit(solution)/shard_map/env_scan/ppermute | solution.py:21
  128.7 14.0 %collective-permute-start.20 = (f32[2,2,128,128]{3,2,0,1:T(8,128)S(1)}, f32[2,2,128,128]{3,2,0,1:T(8,128)S(1)}, u32[]{:S(2)}, u32[]{:S(2)}) collective-permute-start(f32[2,2,128,128]{3,2,0,1:T(8,128)S(1)} %multiply_add_fusion.1), channel_id=1, source_target_pairs={{128,0},{136,8},{144,16},{152,24},{160,32},{168,40},{176,48},{184,... | collective-permute-start | bytes 786440 | tf_op jit(solution)/shard_map/env_scan/ppermute | solution.py:21
  130.0 5.6 %collective-permute-start.14 = (f32[2,2,128]{2,1,0:T(2,128)S(1)}, f32[2,2,128]{2,1,0:T(2,128)S(1)}, u32[]{:S(2)}, u32[]{:S(2)}) collective-permute-start(f32[2,2,128]{2,1,0:T(2,128)S(1)} %mul.385), channel_id=1, source_target_pairs={{64,0},{72,8},{80,16},{88,24},{96,32},{104,40},{112,48},{120,56},{... | collective-permute-start | bytes 6152 | tf_op jit(solution)/shard_map/env_scan/ppermute | solution.py:21
  142.8 11.4 %collective-permute-start.21 = (f32[2,2,128,128]{3,2,0,1:T(8,128)S(1)}, f32[2,2,128,128]{3,2,0,1:T(8,128)S(1)}, u32[]{:S(2)}, u32[]{:S(2)}) collective-permute-start(f32[2,2,128,128]{3,2,0,1:T(8,128)S(1)} %multiply_add_fusion), channel_id=1, source_target_pairs={{256,0},{264,8},{272,16},{280,24},{288,32},{296,40},{304,48},{312,... | collective-permute-start | bytes 786440 | tf_op jit(solution)/shard_map/env_scan/ppermute | solution.py:21
  144.1 5.2 %collective-permute-start.15 = (f32[2,2,128]{2,1,0:T(2,128)S(1)}, f32[2,2,128]{2,1,0:T(2,128)S(1)}, u32[]{:S(2)}, u32[]{:S(2)}) collective-permute-start(f32[2,2,128]{2,1,0:T(2,128)S(1)} %mul.386), channel_id=1, source_target_pairs={{128,0},{136,8},{144,16},{152,24},{160,32},{168,40},{176,48},{184,... | collective-permute-start | bytes 6152 | tf_op jit(solution)/shard_map/env_scan/ppermute | solution.py:21
  188.9 3.5 %copy-start.1 = (f32[2,16,128,128]{3,2,1,0:T(8,128)S(1)}, f32[2,16,128,128]{3,2,1,0:T(8,128)}, u32[]{:S(2)}) copy-start(f32[2,16,128,128]{3,2,1,0:T(8,128)} %multiply_reduce_fusion.3) | copy-start | bytes 6291460
  (7 other events, 15.3 us)
Sparse Core Ops, SparseCore 0:
  120.4 24.6 all-gather.3
  155.2 33.5 all-gather.5

commit v2 on v1

v2 whole, which is shorter than its diff:
```python
import functools

import jax
import jax.numpy as jnp
from jax import lax
from jax.experimental import pallas as pl
from jax.experimental.pallas import tpu as pltpu
from jax.sharding import PartitionSpec as P

ITERS = 4
HALO = 2

epsilon = 1e-06


def chain_env(terms, rate, reverse):
    count = lax.axis_size("chain")
    shape = terms.shape
    width = shape[-1]
    rows = terms.size // width
    block = rows // count
    spread = lax.all_to_all(terms.reshape(count, block, width), "chain", 0, 0, tiled=True)
    speed = lax.all_to_all(rate.reshape(count, block), "chain", 0, 0, tiled=True)
    if reverse:
        spread, speed = spread[::-1], speed[::-1]
    total = jnp.cumsum(speed, axis=0)
    later = jnp.arange(count)[:, None, None] >= jnp.arange(count)[None, :, None]
    gap = jnp.where(later, total[:, None, :] - total[None, :, :], 0.0)
    weight = jnp.where(later, jnp.exp(-gap), 0.0)
    env = jnp.einsum(
        "ghp,hpc->gpc",
        weight,
        spread.astype(jnp.float32),
        precision=lax.Precision.HIGHEST,
        preferred_element_type=jnp.float32,
    )
    if reverse:
        env = env[::-1]
    back = lax.all_to_all(env.astype(jnp.bfloat16), "chain", 0, 0, tiled=True)
    return back.reshape(shape)


def _sum_all(a):
    return jnp.sum(jnp.sum(a, axis=0, keepdims=True), axis=1, keepdims=True)


def _fold(a):
    return jnp.sum(a.reshape(a.shape[0] // 8, 8, a.shape[1]), axis=0)


def iterate_kernel(
    table_ref, place_ref, psi_ref, left_ref, right_ref, out_ref, cos_ref, vec, image, padded
):
    sectors, side, _ = psi_ref.shape
    envs = left_ref.shape[0]
    shifts = 2 * HALO + 1
    entries = float(sectors * side * side)
    vec[...] = psi_ref[...].astype(jnp.float32)
    rim = jnp.zeros((HALO, side, side), jnp.bfloat16)
    padded[0:HALO] = rim
    padded[HALO + sectors : 2 * HALO + sectors] = rim
    nt = (((1,), (1,)), ((), ()))
    zero = jnp.zeros((8, side), jnp.float32)
    cosine = jnp.zeros((1, 1), jnp.float32)
    for iteration in range(ITERS):
        padded[HALO : HALO + sectors] = vec[...].astype(jnp.bfloat16)

        def apply(s, sums):
            lefts = left_ref[:, s].reshape(envs * side, side)
            parts = [jnp.zeros((side, side), jnp.float32) for _ in range(envs)]
            for t in range(shifts):
                prod = jnp.dot(lefts, padded[s + t], preferred_element_type=jnp.float32)
                prod = prod.astype(jnp.bfloat16).astype(jnp.float32)
                for e in range(envs):
                    piece = prod[e * side : (e + 1) * side]
                    for r in range(envs):
                        coef = table_ref[(r * envs + e) * shifts + t]
                        parts[r] = parts[r] + coef * piece
            y = jnp.zeros((side, side), jnp.float32)
            for r in range(envs):
                high = parts[r].astype(jnp.bfloat16)
                low = (parts[r] - high.astype(jnp.float32)).astype(jnp.bfloat16)
                rt = right_ref[r, s]
                y = y + lax.dot_general(high, rt, nt, preferred_element_type=jnp.float32)
                y = y + lax.dot_general(low, rt, nt, preferred_element_type=jnp.float32)
            image[s] = y
            x = vec[s]
            return (sums[0] + _fold(x * x), sums[1] + _fold(x * y), sums[2] + _fold(y * y))

        sx, sxy, sy = lax.fori_loop(0, sectors, apply, (zero, zero, zero))
        self_dot, cross_dot, image_dot = _sum_all(sx), _sum_all(sxy), _sum_all(sy)
        rayleigh_now = cross_dot / self_dot
        step_size = 0.5 * jnp.sqrt(self_dot / (image_dot + epsilon))

        def step(s, su):
            x = vec[s]
            u = x - step_size * (image[s] - rayleigh_now * x)
            vec[s] = u
            return su + _fold(u * u)

        su = _sum_all(lax.fori_loop(0, sectors, step, zero))
        scale = lax.rsqrt(su / entries + epsilon)

        def norm(s, carry):
            vec[s] = vec[s] * scale
            return carry

        lax.fori_loop(0, sectors, norm, 0)
        cosine = cross_dot * lax.rsqrt(self_dot * (image_dot + epsilon))
    local = out_ref.shape[0]
    out_ref[...] = vec[pl.ds(place_ref[0] * local, local)]
    cos_ref[...] = jnp.broadcast_to(cosine, cos_ref.shape)


def iterate(table, place, psi, left_env, right_env, local):
    sectors, side, _ = psi.shape
    smem = pl.BlockSpec(memory_space=pltpu.SMEM)
    vmem = pl.BlockSpec(memory_space=pltpu.VMEM)
    envs = left_env.shape[0]
    flops = ITERS * sectors * (2 * envs * (2 * HALO + 1) + 4 * envs) * 2 * side**3
    return pl.pallas_call(
        iterate_kernel,
        out_shape=(
            jax.ShapeDtypeStruct((local, side, side), jnp.float32),
            jax.ShapeDtypeStruct((8, 128), jnp.float32),
        ),
        in_specs=[smem, smem, vmem, vmem, vmem],
        out_specs=(vmem, vmem),
        scratch_shapes=[
            pltpu.VMEM((sectors, side, side), jnp.float32),
            pltpu.VMEM((sectors, side, side), jnp.float32),
            pltpu.VMEM((sectors + 2 * HALO, side, side), jnp.bfloat16),
        ],
        compiler_params=pltpu.CompilerParams(vmem_limit_bytes=48 * 1024 * 1024),
        cost_estimate=pl.CostEstimate(
            flops=flops, transcendentals=0, bytes_accessed=psi.size * 2 + 4 * left_env.size
        ),
    )(table, place, psi, left_env, right_env)


def body(
    psi_start,
    left_terms,
    left_rate,
    right_terms,
    right_rate,
    term_left,
    term_right,
    term_shift,
    term_coef,
):
    with jax.named_scope("psi_gather"):
        psi = lax.all_gather(psi_start[0], "sector", axis=0, tiled=True)
    with jax.named_scope("env_chain"):
        left_env = chain_env(left_terms[0], left_rate[0], False)
        right_env = chain_env(right_terms[0], right_rate[0], True)
    with jax.named_scope("env_gather"):
        left_env, right_env = lax.all_gather((left_env, right_env), "sector", axis=1, tiled=True)

    envs = left_env.shape[0]
    with jax.named_scope("term_table"):
        pick_right = (term_right[:, None] == jnp.arange(envs)[None]).astype(jnp.float32)
        pick_left = (term_left[:, None] == jnp.arange(envs)[None]).astype(jnp.float32)
        pick_shift = (term_shift[:, None] == jnp.arange(-HALO, HALO + 1)[None]).astype(jnp.float32)
        table = jnp.sum(
            term_coef[:, None, None, None]
            * pick_right[:, :, None, None]
            * pick_left[:, None, :, None]
            * pick_shift[:, None, None, :],
            axis=0,
        ).reshape(-1)
    local = psi_start.shape[1]
    place = jnp.reshape(lax.axis_index("sector"), (1,)).astype(jnp.int32)
    with jax.named_scope("iterations"):
        mine, cos = iterate(table, place, psi, left_env, right_env, local)
    return (mine[None], jnp.reshape(cos[0, 0], (1,)))


def solution(mesh):
    placed = (
        P("chain", "sector", None, None),
        P("chain", None, "sector", None, None),
        P("chain", None, "sector", None),
        P("chain", None, "sector", None, None),
        P("chain", None, "sector", None),
        P(),
        P(),
        P(),
        P(),
    )
    return jax.shard_map(
        body,
        mesh=mesh,
        in_specs=placed,
        out_specs=(P("chain", "sector", None, None), P("chain")),
        check_vma=False,
    )
```

time: 321 us -> 193 us (0.60); the launches traced: 315 us -> 192 us
  starting transfers between devices: 90.4 us -> 9.32 us
  blocking collectives: 17.9 us -> 96 us
  local copies, waits for them, and re-layouts: 54.9 us -> 6.98 us
  other arithmetic: 43.5 us -> 0.38 us
  matrix products: 43 us -> 0.71 us
  Pallas kernels: 0 us -> 37.9 us
  between operations: 31.2 us -> 14.2 us
  waiting for transfers between devices: 34.3 us -> 26.8 us
    ppermute x22 -> x0, starting transfers between devices: 90.3 us -> none  [chain_scan(): got_gain, got_total = lax.ppermute((gain, total), axis, pairs)]
    all_to_all x0 -> x4, blocking collectives: none -> 74.6 us  [the longest x2 42.4 us: chain_env(): lax.all_to_all(rate.reshape(count, block), 'chain', 0, 0, tiled=True)]
    convert_element_type x4 -> x2, local copies, waits for them, and re-layouts: 45.2 us -> 0.18 us  [chain_env(): back = lax.all_to_all(env.astype(jnp.bfloat16), 'chain', 0, 0, tiled=True)]
    dot_general x12 -> x2, matrix products: 43 us -> 0.71 us  [chain_env(): jnp.einsum('ghp,hpc->gpc', weight, spread.astype(jnp.float32), precision=...]
    pallas_call x0 -> x1, Pallas kernels: none -> 37.9 us  [iterate(): pl.pallas_call(iterate_kernel, out_shape=(jax.ShapeDtypeStruct((local, si...]
    reduce_sum x8 -> x0, other arithmetic: 35.4 us -> none  [the longest x4 28.1 us: body(): jnp.sum(table[:, :, :, None, None, None] * left_products[None].astype(jnp...]
    ppermute x22 -> x0, waiting for transfers between devices: 31 us -> none  [chain_scan(): got_gain, got_total = lax.ppermute((gain, total), axis, pairs)]
    all_to_all x0 -> x2, waiting for transfers between devices: none -> 22.8 us  [chain_env(): lax.all_to_all(terms.reshape(count, block, width), 'chain', 0, 0, tiled=T...]
  transfers between devices with their start and end apart: 24 -> 4, of which waited for: 9 -> 3; matrix products, arithmetic and copies ran while one was open for 12% -> 1% of each run, Pallas kernels for 0% -> 0%
where the time goes in v2:
time: 193 us; the launch traced here: 192 us
  blocking collectives  96 us (50%)
  Pallas kernels  37.9 us (20%)
  waiting for transfers between devices  26.8 us (14%)
  between operations  14.2 us (7%)
  starting transfers between devices  9.32 us (5%)
  local copies, waits for them, and re-layouts  6.98 us (4%)
    all_to_all x2, blocking collectives, chain_env(): lax.all_to_all(rate.reshape(count, block), 'chain', 0, 0, tiled=True)  42.4 us
    pallas_call x1, Pallas kernels, iterate(): pl.pallas_call(iterate_kernel, out_shape=(jax.ShapeDtypeStruct((local, si...  37.9 us
    all_to_all x2, blocking collectives, chain_env(): back = lax.all_to_all(env.astype(jnp.bfloat16), 'chain', 0, 0, tiled=True)  32.2 us
    all_to_all x2, waiting for transfers between devices, chain_env(): lax.all_to_all(terms.reshape(count, block, width), 'chain', 0, 0, tiled=T...  22.8 us
    all_gather x1, blocking collectives, body(): psi = lax.all_gather(psi_start[0], 'sector', axis=0, tiled=True)  21.5 us
    all_to_all x2, starting transfers between devices, chain_env(): lax.all_to_all(terms.reshape(count, block, width), 'chain', 0, 0, tiled=T...  9.24 us
    unnamed x16, local copies, waits for them, and re-layouts  5.06 us
    all_gather x2, waiting for transfers between devices, body(): lax.all_gather((left_env, right_env), 'sector', axis=1, tiled=True)  3.96 us
  transfers between devices with their start and end apart: 4, of which 3 were waited for; matrix products, arithmetic and copies ran while one was open for 1% of the time, Pallas kernels for 0%

profile of v2, /device:TPU:1, one launch (start us, length us, event | category | flops | bytes accessed | tf_op | source)
XLA Modules:
  0.0 192.3 jit_solution(13550881977748338103)
XLA Ops:
  7.2 0.8 all_to_all.28
  7.9 27.8 %all_to_all.44 = f32[64,1,8]{2,1,0:T(1,128)S(1)} all-to-all(f32[64,1,8]{2,1,0:T(1,128)S(1)} %bitcast.23), channel_id=1, replica_groups=mesh['chain'=64,'sector'=8] {'chain'}, dimensions={0} | all-to-all | bytes 4096 | tf_op jit(solution)/shard_map/env_chain/all_to_all | solution.py:23
  35.7 4.6 %all-to-all-start.1 = ((bf16[64,8,128]{2,1,0:T(8,128)(2,1)}), bf16[64,8,128]{2,1,0:T(8,128)(2,1)S(1)}, u32[]{:S(2)}, u32[]{:S(2)}) async-start(bf16[64,8,128]{2,1,0:T(8,128)(2,1)} %bitcast.20), calls=%async_computation.1 | async-start | bytes 262144 | tf_op jit(solution)/shard_map/env_chain/all_to_all | solution.py:22
  40.4 0.1 reduce_window_sum.17
  40.5 0.1 copy.40
  40.6 11.4 %all-to-all-done.1 = bf16[64,8,128]{2,1,0:T(8,128)(2,1)S(1)} async-done(((bf16[64,8,128]{2,1,0:T(8,128)(2,1)}), bf16[64,8,128]{2,1,0:T(8,128)(2,1)S(1)}, u32[]{:S(2)}, u32[]{:S(2)}) %all-to-all-start.1) | async-done | bytes 131104 | tf_op jit(solution)/shard_map/env_chain/all_to_all | solution.py:22
  52.0 0.4 fusion
  52.4 0.1 copy.43
  52.5 16.1 %all_to_all.45 = bf16[64,8,128]{2,1,0:T(8,128)(2,1)} all-to-all(bf16[64,8,128]{2,1,0:T(8,128)(2,1)S(1)} %copy.43), channel_id=1, replica_groups=mesh['chain'=64,'sector'=8] {'chain'}, dimensions={0} | all-to-all | bytes 262144 | tf_op jit(solution)/shard_map/env_chain/all_to_all | solution.py:39
  68.6 0.7 copy-done.3
  69.2 0.1 all_to_all.33
  69.3 14.6 %all_to_all.46 = f32[64,1,8]{2,1,0:T(1,128)S(1)} all-to-all(f32[64,1,8]{2,1,0:T(1,128)S(1)} %bitcast.24), channel_id=1, replica_groups=mesh['chain'=64,'sector'=8] {'chain'}, dimensions={0} | all-to-all | bytes 4096 | tf_op jit(solution)/shard_map/env_chain/all_to_all | solution.py:23
  83.9 4.6 %all-to-all-start.4 = ((bf16[64,8,128]{2,1,0:T(8,128)(2,1)}), bf16[64,8,128]{2,1,0:T(8,128)(2,1)S(1)}, u32[]{:S(2)}, u32[]{:S(2)}) async-start(bf16[64,8,128]{2,1,0:T(8,128)(2,1)} %bitcast.10), calls=%async_computation.4 | async-start | bytes 262144 | tf_op jit(solution)/shard_map/env_chain/all_to_all | solution.py:22
  88.6 0.1 reduce_window_sum.18
  88.7 0.1 copy.45
  88.8 11.4 %all-to-all-done.4 = bf16[64,8,128]{2,1,0:T(8,128)(2,1)S(1)} async-done(((bf16[64,8,128]{2,1,0:T(8,128)(2,1)}), bf16[64,8,128]{2,1,0:T(8,128)(2,1)S(1)}, u32[]{:S(2)}, u32[]{:S(2)}) %all-to-all-start.4) | async-done | bytes 131104 | tf_op jit(solution)/shard_map/env_chain/all_to_all | solution.py:22
  100.2 0.4 convolution_bitcast_fusion
  100.6 0.1 copy.48
  100.7 16.1 %all_to_all.47 = bf16[64,8,128]{2,1,0:T(8,128)(2,1)} all-to-all(bf16[64,8,128]{2,1,0:T(8,128)(2,1)S(1)} %copy.48), channel_id=1, replica_groups=mesh['chain'=64,'sector'=8] {'chain'}, dimensions={0} | all-to-all | bytes 262144 | tf_op jit(solution)/shard_map/env_chain/all_to_all | solution.py:39
  116.9 0.6 copy-done.7
  117.5 0.6 copy-done.5
  118.2 0.6 copy-done.4
  118.8 0.1 compare_convert_fusion
  118.9 0.1 multiply_reduce_fusion
  119.0 0.1 copy.37
  119.1 0.1 reshape.136.table_ref
  119.2 21.5 %all-gather = bf16[1,16,128,128]{3,2,0,1:T(8,128)(2,1)S(1)} all-gather(bf16[1,2,128,128]{3,2,0,1:T(8,128)(2,1)S(1)} %bitcast.25), channel_id=2, replica_groups=mesh['chain'=64,'sector'=8] {'sector'}, dimensions={1}, use_global_device_ids=true | all-gather | bytes 589824 | tf_op jit(solution)/shard_map/psi_gather/all_gather | solution.py:153
  140.6 4.0 %all-gather.6.cloned.1.call-done.right_ref = bf16[2,16,128,128]{3,2,1,0:T(8,128)(2,1)} async-done(((bf16[2,2,128,128]{3,2,1,0:T(8,128)(2,1)}), bf16[2,16,128,128]{3,2,1,0:T(8,128)(2,1)}) %all-gather.6.cloned.1.call-update) | async-done | bytes 1048592 | tf_op jit(solution)/shard_map/env_gather/all_gather | solution.py:158
  144.6 1.2 copy-done
  145.8 1.2 copy-done.1
  147.1 37.9 %iterations.1 = (f32[2,128,128]{2,1,0:T(8,128)}, f32[8,128]{1,0:T(8,128)S(1)}) custom-call(f32[20]{0:T(128)S(1)} %reshape.136.table_ref, s32[1]{0:T(128)} %bitcast.place_ref, bf16[16,128,128]{2,1,0:T(8,128)(2,1)S(1)} %bitcast.17, bf16[2,16,128,128]{3,2,1,0:T(8,128)(2,1)S(1)} %copy-done, bf16[2,16,128,128]{3,2,1,0:T(8,128)(2,1)S(1)} %copy-done.1), custom_call_target="tpu_custom_call" | custom-call | flops 7516192768 | bytes 2621440 | tf_op jit(solution)/shard_map/iterations/pallas_call | solution.py:121
  185.0 0.5 slice.3
  (23 shorter events, 0.2 us)
Async XLA Ops:
  35.7 16.3 %all-to-all-start.1 = ((bf16[64,8,128]{2,1,0:T(8,128)(2,1)}), bf16[64,8,128]{2,1,0:T(8,128)(2,1)S(1)}, u32[]{:S(2)}, u32[]{:S(2)}) async-start(bf16[64,8,128]{2,1,0:T(8,128)(2,1)} %bitcast.20), calls=%async_computation.1 | async-start | bytes 262144 | tf_op jit(solution)/shard_map/env_chain/all_to_all | solution.py:22
  40.3 100.3 %all-gather.4.cloned.1.call-start = ((), (), s32[]{:S(2)}) async-start(), calls=%async_computation.6 | async-start | bytes 1179648 | tf_op jit(solution)/shard_map/env_gather/all_gather | solution.py:158
  68.5 0.7 copy-start.3
  83.9 16.2 %all-to-all-start.4 = ((bf16[64,8,128]{2,1,0:T(8,128)(2,1)}), bf16[64,8,128]{2,1,0:T(8,128)(2,1)S(1)}, u32[]{:S(2)}, u32[]{:S(2)}) async-start(bf16[64,8,128]{2,1,0:T(8,128)(2,1)} %bitcast.10), calls=%async_computation.4 | async-start | bytes 262144 | tf_op jit(solution)/shard_map/env_chain/all_to_all | solution.py:22
  88.6 56.0 %all-gather.6.cloned.1.call-start = ((), (), s32[]{:S(2)}) async-start(), calls=%async_computation.7 | async-start | bytes 1179648 | tf_op jit(solution)/shard_map/env_gather/all_gather | solution.py:158
  116.8 2.4 %copy-start.2 = (bf16[1,2,128,128]{3,2,1,0:T(8,128)(2,1)S(1)}, bf16[1,2,128,128]{3,2,1,0:T(8,128)(2,1)}, u32[]{:S(2)}) copy-start(bf16[1,2,128,128]{3,2,1,0:T(8,128)(2,1)} %param.9) | copy-start | bytes 196612
  116.8 0.7 copy-start.7
  117.5 0.7 copy-start.5
  117.5 0.7 copy-start.6
  118.2 0.7 copy-start.4
  144.6 1.2 copy-start
  145.8 1.2 copy-start.1
Sparse Core Ops, SparseCore 0:
  68.7 24.1 all-gather.3
  116.9 27.6 all-gather.5

commit v3 on v2

--- a/solution.py
+++ b/solution.py
@@ -13,31 +13,40 @@
 epsilon = 1e-06
 
 
-def chain_env(terms, rate, reverse):
+def chain_envs(left_terms, left_rate, right_terms, right_rate):
     count = lax.axis_size("chain")
-    shape = terms.shape
+    shape = left_terms.shape
     width = shape[-1]
-    rows = terms.size // width
-    block = rows // count
-    spread = lax.all_to_all(terms.reshape(count, block, width), "chain", 0, 0, tiled=True)
-    speed = lax.all_to_all(rate.reshape(count, block), "chain", 0, 0, tiled=True)
-    if reverse:
-        spread, speed = spread[::-1], speed[::-1]
-    total = jnp.cumsum(speed, axis=0)
-    later = jnp.arange(count)[:, None, None] >= jnp.arange(count)[None, :, None]
-    gap = jnp.where(later, total[:, None, :] - total[None, :, :], 0.0)
-    weight = jnp.where(later, jnp.exp(-gap), 0.0)
+    block = left_terms.size // width // count
+    packed = jnp.concatenate(
+        [left_terms.reshape(count, block, width), right_terms.reshape(count, block, width)], axis=1
+    )
+    spread = lax.all_to_all(packed, "chain", 0, 0, tiled=True).astype(jnp.float32)
+    rates = lax.all_gather(
+        jnp.stack([left_rate.reshape(count, block), right_rate.reshape(count, block)]), "chain"
+    )
+    mine = lax.axis_index("chain")
+    speed = lax.dynamic_index_in_dim(rates, mine, 2, keepdims=False)
+    ahead = jnp.cumsum(speed[:, 0], axis=0)
+    behind = jnp.cumsum(speed[::-1, 1], axis=0)[::-1]
+    order = jnp.arange(count)
+    later = (order[:, None] >= order[None, :])[:, :, None]
+    earlier = (order[:, None] <= order[None, :])[:, :, None]
+    forward = jnp.where(later, ahead[:, None, :] - ahead[None, :, :], 0.0)
+    backward = jnp.where(earlier, behind[:, None, :] - behind[None, :, :], 0.0)
+    weight = jnp.concatenate(
+        [jnp.where(later, jnp.exp(-forward), 0.0), jnp.where(earlier, jnp.exp(-backward), 0.0)],
+        axis=2,
+    )
     env = jnp.einsum(
         "ghp,hpc->gpc",
         weight,
-        spread.astype(jnp.float32),
+        spread,
         precision=lax.Precision.HIGHEST,
         preferred_element_type=jnp.float32,
     )
-    if reverse:
-        env = env[::-1]
     back = lax.all_to_all(env.astype(jnp.bfloat16), "chain", 0, 0, tiled=True)
-    return back.reshape(shape)
+    return back[:, :block].reshape(shape), back[:, block:].reshape(shape)
 
 
 def _sum_all(a):
@@ -152,8 +161,7 @@
     with jax.named_scope("psi_gather"):
         psi = lax.all_gather(psi_start[0], "sector", axis=0, tiled=True)
     with jax.named_scope("env_chain"):
-        left_env = chain_env(left_terms[0], left_rate[0], False)
-        right_env = chain_env(right_terms[0], right_rate[0], True)
+        left_env, right_env = chain_envs(left_terms[0], left_rate[0], right_terms[0], right_rate[0])
     with jax.named_scope("env_gather"):
         left_env, right_env = lax.all_gather((left_env, right_env), "sector", axis=1, tiled=True)
 

time: 193 us -> 205 us (1.062)
  waiting for transfers between devices: 26.8 us -> 36.3 us
  blocking collectives: 96 us -> 87.7 us
  starting transfers between devices: 9.32 us -> 17.2 us
    all_to_all x4 -> x1, blocking collectives: 74.6 us -> 21.3 us  [chain_envs(): back = lax.all_to_all(env.astype(jnp.bfloat16), 'chain', 0, 0, tiled=True)]
    all_gather x0 -> x1, blocking collectives: none -> 39.6 us  [chain_envs(): lax.all_gather(jnp.stack([left_rate.reshape(count, block), right_rate.res...]
    all_gather x2, waiting for transfers between devices: 3.96 us -> 35.6 us  [body(): lax.all_gather((left_env, right_env), 'sector', axis=1, tiled=True)]
    all_to_all x2 -> x1, waiting for transfers between devices: 22.8 us -> 0.01 us  [chain_envs(): lax.all_to_all(packed, 'chain', 0, 0, tiled=True).astype(jnp.float32)]
    all_to_all x2 -> x1, starting transfers between devices: 9.24 us -> 17.1 us  [chain_envs(): lax.all_to_all(packed, 'chain', 0, 0, tiled=True).astype(jnp.float32)]
    all_gather x1, blocking collectives: 21.5 us -> 26.9 us  [body(): psi = lax.all_gather(psi_start[0], 'sector', axis=0, tiled=True)]
    unnamed x16 -> x18, local copies, waits for them, and re-layouts: 5.06 us -> 5.7 us
  transfers between devices with their start and end apart: 4 -> 3, of which waited for: 3 -> 2; matrix products, arithmetic and copies ran while one was open for 1% -> 1% of each run, Pallas kernels for 0% -> 0%
where the time goes in v3:
time: 205 us
  blocking collectives  87.7 us (43%)
  Pallas kernels  38.1 us (19%)
  waiting for transfers between devices  36.3 us (18%)
  starting transfers between devices  17.2 us (8%)
  between operations  14.2 us (7%)
  local copies, waits for them, and re-layouts  8.73 us (4%)
  other arithmetic  2.35 us (1%)
    all_gather x1, blocking collectives, chain_envs(): lax.all_gather(jnp.stack([left_rate.reshape(count, block), right_rate.res...  39.6 us
    pallas_call x1, Pallas kernels, iterate(): pl.pallas_call(iterate_kernel, out_shape=(jax.ShapeDtypeStruct((local, si...  38.1 us
    all_gather x2, waiting for transfers between devices, body(): lax.all_gather((left_env, right_env), 'sector', axis=1, tiled=True)  35.6 us
    all_gather x1, blocking collectives, body(): psi = lax.all_gather(psi_start[0], 'sector', axis=0, tiled=True)  26.9 us
    all_to_all x1, blocking collectives, chain_envs(): back = lax.all_to_all(env.astype(jnp.bfloat16), 'chain', 0, 0, tiled=True)  21.3 us
    all_to_all x1, starting transfers between devices, chain_envs(): lax.all_to_all(packed, 'chain', 0, 0, tiled=True).astype(jnp.float32)  17.1 us
    unnamed x18, local copies, waits for them, and re-layouts  5.7 us
  transfers between devices with their start and end apart: 3, of which 2 were waited for; matrix products, arithmetic and copies ran while one was open for 1% of the time, Pallas kernels for 0%

profile of v3, /device:TPU:1, one launch (start us, length us, event | category | flops | bytes accessed | tf_op | source)
XLA Modules:
  0.0 205.0 jit_solution(14759833803955124831)
XLA Ops:
  7.2 1.7 pad_maximum_fusion
  8.9 17.1 %all-to-all-start = ((bf16[64,16,128]{2,1,0:T(8,128)(2,1)}), bf16[64,16,128]{2,1,0:T(8,128)(2,1)S(1)}, u32[]{:S(2)}, u32[]{:S(2)}) async-start(bf16[64,16,128]{2,1,0:T(8,128)(2,1)} %pad_maximum_fusion), calls=%async_computation | async-start | bytes 524288 | tf_op jit(solution)/shard_map/env_chain/all_to_all | solution.py:24
  26.1 0.7 copy-done.3
  26.8 0.1 squeeze.28
  26.9 0.6 copy-done.4
  27.5 0.1 squeeze.29
  27.7 39.6 %all-gather.1 = f32[128,64,8]{1,2,0:T(8,128)S(1)} all-gather(f32[2,64,8]{1,2,0:T(8,128)S(1)} %pad_maximum_fusion.1), channel_id=3, replica_groups=mesh['chain'=64,'sector'=8] {'chain'}, dimensions={0}, use_global_device_ids=true | all-gather | bytes 266240 | tf_op jit(solution)/shard_map/env_chain/all_gather | solution.py:25
  67.3 0.2 constant_dynamic-slice_fusion
  67.5 0.8 copy.41
  68.3 0.1 reduce_window_sum.17
  68.5 0.1 reduce_window_sum.18
  68.6 0.1 copy.44
  68.7 0.2 exponential_select_fusion
  68.9 0.4 fusion
  69.4 0.2 copy.47
  69.5 21.3 %all_to_all.10 = bf16[64,16,128]{2,1,0:T(8,128)(2,1)S(1)} all-to-all(bf16[64,16,128]{2,1,0:T(8,128)(2,1)S(1)} %copy.47), channel_id=1, replica_groups=mesh['chain'=64,'sector'=8] {'chain'}, dimensions={0} | all-to-all | bytes 524288 | tf_op jit(solution)/shard_map/env_chain/all_to_all | solution.py:48
  90.8 0.7 fusion.6
  91.6 0.7 all-gather.7.cloned.1.call-update
  92.3 0.6 copy-done.8
  93.0 0.6 copy-done.6
  93.6 0.6 copy-done.5
  94.3 0.1 compare_convert_fusion
  94.4 0.1 multiply_reduce_fusion
  94.5 0.1 copy.37
  94.6 0.1 reshape.139.table_ref
  94.6 26.9 %all-gather = bf16[1,16,128,128]{3,2,0,1:T(8,128)(2,1)S(1)} all-gather(bf16[1,2,128,128]{3,2,0,1:T(8,128)(2,1)S(1)} %bitcast.24), channel_id=2, replica_groups=mesh['chain'=64,'sector'=8] {'sector'}, dimensions={1}, use_global_device_ids=true | all-gather | bytes 589824 | tf_op jit(solution)/shard_map/psi_gather/all_gather | solution.py:162
  121.5 4.1 %all-gather.5.cloned.1.call-done.left_ref = bf16[2,16,128,128]{3,2,1,0:T(8,128)(2,1)} async-done(((bf16[2,2,128,128]{3,2,1,0:T(8,128)(2,1)}), bf16[2,16,128,128]{3,2,1,0:T(8,128)(2,1)}) %all-gather.5.cloned.1.call-update) | async-done | bytes 1048592 | tf_op jit(solution)/shard_map/env_gather/all_gather | solution.py:166
  125.6 31.5 %all-gather.7.cloned.1.call-done.right_ref = bf16[2,16,128,128]{3,2,1,0:T(8,128)(2,1)} async-done(((bf16[2,2,128,128]{3,2,1,0:T(8,128)(2,1)}), bf16[2,16,128,128]{3,2,1,0:T(8,128)(2,1)}) %all-gather.7.cloned.1.call-update) | async-done | bytes 1048592 | tf_op jit(solution)/shard_map/env_gather/all_gather | solution.py:166
  157.1 1.2 copy-done
  158.3 1.2 copy-done.1
  159.6 38.1 %iterations.1 = (f32[2,128,128]{2,1,0:T(8,128)}, f32[8,128]{1,0:T(8,128)S(1)}) custom-call(f32[20]{0:T(128)S(1)} %reshape.139.table_ref, s32[1]{0:T(128)} %bitcast.place_ref, bf16[16,128,128]{2,1,0:T(8,128)(2,1)S(1)} %bitcast.16, bf16[2,16,128,128]{3,2,1,0:T(8,128)(2,1)S(1)} %copy-done, bf16[2,16,128,128]{3,2,1,0:T(8,128)(2,1)S(1)} %copy-done.1), custom_call_target="tpu_custom_call" | custom-call | flops 7516192768 | bytes 2621440 | tf_op jit(solution)/shard_map/iterations/pallas_call | solution.py:130
  197.6 0.5 slice.19
  (28 shorter events, 0.4 us)
Async XLA Ops:
  8.9 60.0 %all-to-all-start = ((bf16[64,16,128]{2,1,0:T(8,128)(2,1)}), bf16[64,16,128]{2,1,0:T(8,128)(2,1)S(1)}, u32[]{:S(2)}, u32[]{:S(2)}) async-start(bf16[64,16,128]{2,1,0:T(8,128)(2,1)} %pad_maximum_fusion), calls=%async_computation | async-start | bytes 524288 | tf_op jit(solution)/shard_map/env_chain/all_to_all | solution.py:24
  26.0 99.6 %all-gather.5.cloned.1.call-start = ((), (), s32[]{:S(2)}) async-start(), calls=%async_computation.2 | async-start | bytes 1179648 | tf_op jit(solution)/shard_map/env_gather/all_gather | solution.py:166
  26.1 0.7 copy-start.3
  26.9 0.7 copy-start.4
  91.6 65.6 %all-gather.7.cloned.1.call-start = ((), (), s32[]{:S(2)}) async-start(), calls=%async_computation.3 | async-start | bytes 1179648 | tf_op jit(solution)/shard_map/env_gather/all_gather | solution.py:166
  91.6 3.0 %copy-start.2 = (bf16[1,2,128,128]{3,2,1,0:T(8,128)(2,1)S(1)}, bf16[1,2,128,128]{3,2,1,0:T(8,128)(2,1)}, u32[]{:S(2)}) copy-start(bf16[1,2,128,128]{3,2,1,0:T(8,128)(2,1)} %param.9) | copy-start | bytes 196612
  92.3 0.7 copy-start.8
  93.0 0.7 copy-start.6
  93.0 0.7 copy-start.7
  93.6 0.7 copy-start.5
  157.1 1.2 copy-start
  158.3 1.2 copy-start.1
Sparse Core Ops, SparseCore 0:
  91.7 33.8 all-gather.4
  128.3 28.7 all-gather.6

commit v4 on v3

--- a/solution.py
+++ b/solution.py
@@ -18,15 +18,25 @@
     shape = left_terms.shape
     width = shape[-1]
     block = left_terms.size // width // count
+    rates = jnp.stack([left_rate.reshape(count, block), right_rate.reshape(count, block)], axis=1)
+    pieces = []
+    rest = rates
+    for _ in range(3):
+        piece = rest.astype(jnp.bfloat16)
+        rest = rest - piece.astype(jnp.float32)
+        pieces.append(piece)
+    coded = jnp.stack(pieces, axis=1).reshape(count, 6 * block)
+    coded = jnp.pad(coded, ((0, 0), (0, 2 * block * width - 6 * block)))
+    coded = coded.reshape(count, 2 * block, width)
     packed = jnp.concatenate(
-        [left_terms.reshape(count, block, width), right_terms.reshape(count, block, width)], axis=1
-    )
-    spread = lax.all_to_all(packed, "chain", 0, 0, tiled=True).astype(jnp.float32)
-    rates = lax.all_gather(
-        jnp.stack([left_rate.reshape(count, block), right_rate.reshape(count, block)]), "chain"
-    )
-    mine = lax.axis_index("chain")
-    speed = lax.dynamic_index_in_dim(rates, mine, 2, keepdims=False)
+        [left_terms.reshape(count, block, width), right_terms.reshape(count, block, width), coded],
+        axis=1,
+    )
+    spread = lax.all_to_all(packed, "chain", 0, 0, tiled=True)
+    got = spread[:, 2 * block :].reshape(count, 2 * block * width)[:, : 6 * block]
+    got = got.astype(jnp.float32).reshape(count, 3, 2, block)
+    speed = (got[:, 0] + got[:, 1]) + got[:, 2]
+    spread = spread[:, : 2 * block].astype(jnp.float32)
     ahead = jnp.cumsum(speed[:, 0], axis=0)
     behind = jnp.cumsum(speed[::-1, 1], axis=0)[::-1]
     order = jnp.arange(count)
@@ -57,14 +67,12 @@
     return jnp.sum(a.reshape(a.shape[0] // 8, 8, a.shape[1]), axis=0)
 
 
-def iterate_kernel(
-    table_ref, place_ref, psi_ref, left_ref, right_ref, out_ref, cos_ref, vec, image, padded
-):
-    sectors, side, _ = psi_ref.shape
-    envs = left_ref.shape[0]
+def iterate_kernel(table_ref, place_ref, stack_ref, out_ref, cos_ref, vec, image, padded):
+    _, sectors, side, _ = stack_ref.shape
+    envs = (stack_ref.shape[0] - 1) // 2
     shifts = 2 * HALO + 1
     entries = float(sectors * side * side)
-    vec[...] = psi_ref[...].astype(jnp.float32)
+    vec[...] = stack_ref[2 * envs].astype(jnp.float32)
     rim = jnp.zeros((HALO, side, side), jnp.bfloat16)
     padded[0:HALO] = rim
     padded[HALO + sectors : 2 * HALO + sectors] = rim
@@ -75,7 +83,7 @@
         padded[HALO : HALO + sectors] = vec[...].astype(jnp.bfloat16)
 
         def apply(s, sums):
-            lefts = left_ref[:, s].reshape(envs * side, side)
+            lefts = stack_ref[0:envs, s].reshape(envs * side, side)
             parts = [jnp.zeros((side, side), jnp.float32) for _ in range(envs)]
             for t in range(shifts):
                 prod = jnp.dot(lefts, padded[s + t], preferred_element_type=jnp.float32)
@@ -89,7 +97,7 @@
             for r in range(envs):
                 high = parts[r].astype(jnp.bfloat16)
                 low = (parts[r] - high.astype(jnp.float32)).astype(jnp.bfloat16)
-                rt = right_ref[r, s]
+                rt = stack_ref[envs + r, s]
                 y = y + lax.dot_general(high, rt, nt, preferred_element_type=jnp.float32)
                 y = y + lax.dot_general(low, rt, nt, preferred_element_type=jnp.float32)
             image[s] = y
@@ -121,11 +129,11 @@
     cos_ref[...] = jnp.broadcast_to(cosine, cos_ref.shape)
 
 
-def iterate(table, place, psi, left_env, right_env, local):
-    sectors, side, _ = psi.shape
+def iterate(table, place, stack, local):
+    _, sectors, side, _ = stack.shape
     smem = pl.BlockSpec(memory_space=pltpu.SMEM)
     vmem = pl.BlockSpec(memory_space=pltpu.VMEM)
-    envs = left_env.shape[0]
+    envs = (stack.shape[0] - 1) // 2
     flops = ITERS * sectors * (2 * envs * (2 * HALO + 1) + 4 * envs) * 2 * side**3
     return pl.pallas_call(
         iterate_kernel,
@@ -133,7 +141,7 @@
             jax.ShapeDtypeStruct((local, side, side), jnp.float32),
             jax.ShapeDtypeStruct((8, 128), jnp.float32),
         ),
-        in_specs=[smem, smem, vmem, vmem, vmem],
+        in_specs=[smem, smem, vmem],
         out_specs=(vmem, vmem),
         scratch_shapes=[
             pltpu.VMEM((sectors, side, side), jnp.float32),
@@ -142,9 +150,9 @@
         ],
         compiler_params=pltpu.CompilerParams(vmem_limit_bytes=48 * 1024 * 1024),
         cost_estimate=pl.CostEstimate(
-            flops=flops, transcendentals=0, bytes_accessed=psi.size * 2 + 4 * left_env.size
+            flops=flops, transcendentals=0, bytes_accessed=stack.size * 2 + 4 * local * side * side
         ),
-    )(table, place, psi, left_env, right_env)
+    )(table, place, stack)
 
 
 def body(
@@ -158,14 +166,14 @@
     term_shift,
     term_coef,
 ):
-    with jax.named_scope("psi_gather"):
-        psi = lax.all_gather(psi_start[0], "sector", axis=0, tiled=True)
     with jax.named_scope("env_chain"):
         left_env, right_env = chain_envs(left_terms[0], left_rate[0], right_terms[0], right_rate[0])
     with jax.named_scope("env_gather"):
-        left_env, right_env = lax.all_gather((left_env, right_env), "sector", axis=1, tiled=True)
-
-    envs = left_env.shape[0]
+        stack = lax.all_gather(
+            jnp.concatenate([left_env, right_env, psi_start], axis=0), "sector", axis=1, tiled=True
+        )
+
+    envs = left_terms.shape[1]
     with jax.named_scope("term_table"):
         pick_right = (term_right[:, None] == jnp.arange(envs)[None]).astype(jnp.float32)
         pick_left = (term_left[:, None] == jnp.arange(envs)[None]).astype(jnp.float32)
@@ -180,7 +188,7 @@
     local = psi_start.shape[1]
     place = jnp.reshape(lax.axis_index("sector"), (1,)).astype(jnp.int32)
     with jax.named_scope("iterations"):
-        mine, cos = iterate(table, place, psi, left_env, right_env, local)
+        mine, cos = iterate(table, place, stack, local)
     return (mine[None], jnp.reshape(cos[0, 0], (1,)))
 
 

time: 205 us -> 142 us (0.69)
  blocking collectives: 87.7 us -> 20.1 us
  waiting for transfers between devices: 36.3 us -> 42.7 us
  local copies, waits for them, and re-layouts: 8.73 us -> 5.42 us
    all_gather x2 -> x0, blocking collectives: 66.4 us -> none  [the longest x1 39.6 us: chain_envs(): lax.all_gather(jnp.stack([left_rate.reshape(count, block), right_rate.res...]
    all_to_all x1, waiting for transfers between devices: 0.01 us -> 16.3 us  [chain_envs(): spread = lax.all_to_all(packed, 'chain', 0, 0, tiled=True)]
    all_gather x2 -> x1, waiting for transfers between devices: 35.6 us -> 26.4 us  [body(): lax.all_gather(jnp.concatenate([left_env, right_env, psi_start], axis=0),...]
    unnamed x18 -> x12, local copies, waits for them, and re-layouts: 5.7 us -> 1.77 us
  transfers between devices with their start and end apart: 3 -> 2, of which waited for: 2 -> 2; matrix products, arithmetic and copies ran while one was open for 1% -> 0% of each run, Pallas kernels for 0% -> 0%
where the time goes in v4:
time: 142 us; the launch traced here: 141 us
  waiting for transfers between devices  42.7 us (30%)
  Pallas kernels  38.1 us (27%)
  blocking collectives  20.1 us (14%)
  starting transfers between devices  17.2 us (12%)
  between operations  14.3 us (10%)
  local copies, waits for them, and re-layouts  5.42 us (4%)
  other arithmetic  3.27 us (2%)
    pallas_call x1, Pallas kernels, iterate(): pl.pallas_call(iterate_kernel, out_shape=(jax.ShapeDtypeStruct((local, si...  38.1 us
    all_gather x1, waiting for transfers between devices, body(): lax.all_gather(jnp.concatenate([left_env, right_env, psi_start], axis=0),...  26.4 us
    all_to_all x1, blocking collectives, chain_envs(): back = lax.all_to_all(env.astype(jnp.bfloat16), 'chain', 0, 0, tiled=True)  20.1 us
    all_to_all x1, starting transfers between devices, chain_envs(): spread = lax.all_to_all(packed, 'chain', 0, 0, tiled=True)  17.1 us
    all_to_all x1, waiting for transfers between devices, chain_envs(): spread = lax.all_to_all(packed, 'chain', 0, 0, tiled=True)  16.3 us
  transfers between devices with their start and end apart: 2, of which 2 were waited for; matrix products, arithmetic and copies ran while one was open for 0% of the time, Pallas kernels for 0%

profile of v4, /device:TPU:1, one launch (start us, length us, event | category | flops | bytes accessed | tf_op | source)
XLA Modules:
  0.0 141.4 jit_solution(8436522067184518348)
XLA Ops:
  7.2 0.8 stack.13
  7.9 0.1 copy.58
  8.0 0.8 stack.14
  8.8 0.1 copy.59
  8.9 0.1 pad.4
  9.0 0.3 copy.70
  9.2 1.8 %pad_maximum_fusion = bf16[64,32,128]{2,1,0:T(8,128)(2,1)} fusion(bf16[64,16,128]{2,1,0:T(8,128)(2,1)S(1)} %copy.70, bf16[64,8,128]{2,1,0:T(8,128)(2,1)} %bitcast.23, bf16[64,8,128]{2,1,0:T(8,128)(2,1)} %bitcast.24), kind=kLoop, calls=%fused_computation.2 | loop fusion | flops 1572864 | bytes 1048576 | tf_op jit(solution)/shard_map/env_chain/concatenate | solution.py:31
  11.1 17.1 %all-to-all-start = ((bf16[64,32,128]{2,1,0:T(8,128)(2,1)}), bf16[64,32,128]{2,1,0:T(8,128)(2,1)S(1)}, u32[]{:S(2)}, u32[]{:S(2)}) async-start(bf16[64,32,128]{2,1,0:T(8,128)(2,1)} %pad_maximum_fusion), calls=%async_computation | async-start | bytes 1048576 | tf_op jit(solution)/shard_map/env_chain/all_to_all | solution.py:35
  28.2 0.0 all-gather.2.cloned.1.call-start
  28.3 16.3 %all-to-all-done = bf16[64,32,128]{2,1,0:T(8,128)(2,1)S(1)} async-done(((bf16[64,32,128]{2,1,0:T(8,128)(2,1)}), bf16[64,32,128]{2,1,0:T(8,128)(2,1)S(1)}, u32[]{:S(2)}, u32[]{:S(2)}) %all-to-all-start) | async-done | bytes 524320 | tf_op jit(solution)/shard_map/env_chain/all_to_all | solution.py:35
  44.7 0.3 copy.71
  45.0 0.1 rev.6
  45.1 0.1 copy.66
  45.2 0.1 reduce_window_sum.18
  45.3 0.1 copy.67
  45.4 0.1 copy.63
  45.5 0.1 reduce_window_sum.17
  45.6 0.1 copy.64
  45.6 0.2 exponential_select_fusion
  45.9 0.4 fusion
  46.3 0.2 copy.69
  46.5 20.1 %all_to_all.10 = bf16[64,16,128]{2,1,0:T(8,128)(2,1)S(1)} all-to-all(bf16[64,16,128]{2,1,0:T(8,128)(2,1)S(1)} %copy.69), channel_id=1, replica_groups=mesh['chain'=64,'sector'=8] {'chain'}, dimensions={0} | all-to-all | bytes 524288 | tf_op jit(solution)/shard_map/env_chain/all_to_all | solution.py:58
  66.6 0.8 pad_maximum_fusion.1
  67.4 0.0 all-gather.2.cloned.1.call-update
  67.5 0.1 compare_convert_fusion
  67.6 0.1 multiply_reduce_fusion
  67.6 0.1 copy.57
  67.7 0.1 reshape.273.table_ref
  67.8 26.4 %all-gather.2.cloned.1.call-done.stack_ref = bf16[5,16,128,128]{3,2,1,0:T(8,128)(2,1)} async-done(((bf16[5,2,128,128]{3,2,1,0:T(8,128)(2,1)}), bf16[5,16,128,128]{3,2,1,0:T(8,128)(2,1)}) %all-gather.2.cloned.1.call-update) | async-done | bytes 2621456 | tf_op jit(solution)/shard_map/env_gather/all_gather | solution.py:172
  94.2 1.7 %copy-done = bf16[5,16,128,128]{3,2,1,0:T(8,128)(2,1)S(1)} copy-done((bf16[5,16,128,128]{3,2,1,0:T(8,128)(2,1)S(1)}, bf16[5,16,128,128]{3,2,1,0:T(8,128)(2,1)}, u32[]{:S(2)}) %copy-start) | copy-done | bytes 2621464
  96.0 38.1 %iterations.1 = (f32[2,128,128]{2,1,0:T(8,128)}, f32[8,128]{1,0:T(8,128)S(1)}) custom-call(f32[20]{0:T(128)S(1)} %reshape.273.table_ref, s32[1]{0:T(128)} %bitcast.place_ref, bf16[5,16,128,128]{3,2,1,0:T(8,128)(2,1)S(1)} %copy-done), custom_call_target="tpu_custom_call" | custom-call | flops 7516192768 | bytes 2752512 | tf_op jit(solution)/shard_map/iterations/pallas_call | solution.py:138
  134.0 0.5 slice.43
  (27 shorter events, 0.2 us)
Async XLA Ops:
  11.1 33.5 %all-to-all-start = ((bf16[64,32,128]{2,1,0:T(8,128)(2,1)}), bf16[64,32,128]{2,1,0:T(8,128)(2,1)S(1)}, u32[]{:S(2)}, u32[]{:S(2)}) async-start(bf16[64,32,128]{2,1,0:T(8,128)(2,1)} %pad_maximum_fusion), calls=%async_computation | async-start | bytes 1048576 | tf_op jit(solution)/shard_map/env_chain/all_to_all | solution.py:35
  28.2 66.0 %all-gather.2.cloned.1.call-start = ((), (), s32[]{:S(2)}) async-start(), calls=%async_computation.2 | async-start | bytes 2949120 | tf_op jit(solution)/shard_map/env_gather/all_gather | solution.py:172
  28.3 38.3 %copy-start.1 = (bf16[1,2,128,128]{3,2,1,0:T(8,128)(2,1)S(1)}, bf16[1,2,128,128]{3,2,1,0:T(8,128)(2,1)}, u32[]{:S(2)}) copy-start(bf16[1,2,128,128]{3,2,1,0:T(8,128)(2,1)} %param.9) | copy-start | bytes 196612
  44.6 22.8 %copy-start.5 = (s32[12]{0:T(128)S(1)}, s32[12]{0:T(128)}, u32[]{:S(2)}) copy-start(s32[12]{0:T(128)} %param.14) | copy-start | bytes 148
  44.6 22.8 %copy-start.3 = (f32[12]{0:T(128)S(1)}, f32[12]{0:T(128)}, u32[]{:S(2)}) copy-start(f32[12]{0:T(128)} %param.17) | copy-start | bytes 148
  44.6 22.8 %copy-start.4 = (s32[12]{0:T(128)S(1)}, s32[12]{0:T(128)}, u32[]{:S(2)}) copy-start(s32[12]{0:T(128)} %param.15) | copy-start | bytes 148
  44.7 22.8 %copy-start.2 = (s32[12]{0:T(128)S(1)}, s32[12]{0:T(128)}, u32[]{:S(2)}) copy-start(s32[12]{0:T(128)} %param.16) | copy-start | bytes 148
  94.2 1.7 %copy-start = (bf16[5,16,128,128]{3,2,1,0:T(8,128)(2,1)S(1)}, bf16[5,16,128,128]{3,2,1,0:T(8,128)(2,1)}, u32[]{:S(2)}) copy-start(bf16[5,16,128,128]{3,2,1,0:T(8,128)(2,1)} %all-gather.2.cloned.1.call-done.stack_ref) | copy-start | bytes 7864324
Sparse Core Ops, SparseCore 0:
  67.5 26.6 all-gather.1

commit v5 on v4

--- a/solution.py
+++ b/solution.py
@@ -22,9 +22,9 @@
     pieces = []
     rest = rates
     for _ in range(3):
-        piece = rest.astype(jnp.bfloat16)
-        rest = rest - piece.astype(jnp.float32)
-        pieces.append(piece)
+        piece = lax.reduce_precision(rest, exponent_bits=8, mantissa_bits=7)
+        rest = rest - piece
+        pieces.append(piece.astype(jnp.bfloat16))
     coded = jnp.stack(pieces, axis=1).reshape(count, 6 * block)
     coded = jnp.pad(coded, ((0, 0), (0, 2 * block * width - 6 * block)))
     coded = coded.reshape(count, 2 * block, width)
@@ -67,39 +67,49 @@
     return jnp.sum(a.reshape(a.shape[0] // 8, 8, a.shape[1]), axis=0)
 
 
-def iterate_kernel(table_ref, place_ref, stack_ref, out_ref, cos_ref, vec, image, padded):
+def iterate_kernel(table_ref, place_ref, stack_ref, out_ref, cos_ref, vec, image, diag):
     _, sectors, side, _ = stack_ref.shape
     envs = (stack_ref.shape[0] - 1) // 2
     shifts = 2 * HALO + 1
     entries = float(sectors * side * side)
     vec[...] = stack_ref[2 * envs].astype(jnp.float32)
-    rim = jnp.zeros((HALO, side, side), jnp.bfloat16)
-    padded[0:HALO] = rim
-    padded[HALO + sectors : 2 * HALO + sectors] = rim
-    nt = (((1,), (1,)), ((), ()))
+    diag[...] = jnp.zeros(diag.shape, jnp.bfloat16)
     zero = jnp.zeros((8, side), jnp.float32)
     cosine = jnp.zeros((1, 1), jnp.float32)
     for iteration in range(ITERS):
-        padded[HALO : HALO + sectors] = vec[...].astype(jnp.bfloat16)
+
+        def fill(s, carry):
+            w = vec[s].astype(jnp.bfloat16)
+            for e in range(envs):
+                diag[s + HALO, e * side : (e + 1) * side, e * side : (e + 1) * side] = w
+            return carry
+
+        lax.fori_loop(0, sectors, fill, 0)
 
         def apply(s, sums):
-            lefts = stack_ref[0:envs, s].reshape(envs * side, side)
+            lefts = jnp.concatenate([stack_ref[e, s] for e in range(envs)], axis=1)
             parts = [jnp.zeros((side, side), jnp.float32) for _ in range(envs)]
             for t in range(shifts):
-                prod = jnp.dot(lefts, padded[s + t], preferred_element_type=jnp.float32)
+                prod = jnp.dot(lefts, diag[s + t], preferred_element_type=jnp.float32)
                 prod = prod.astype(jnp.bfloat16).astype(jnp.float32)
                 for e in range(envs):
-                    piece = prod[e * side : (e + 1) * side]
+                    piece = prod[:, e * side : (e + 1) * side]
                     for r in range(envs):
                         coef = table_ref[(r * envs + e) * shifts + t]
                         parts[r] = parts[r] + coef * piece
-            y = jnp.zeros((side, side), jnp.float32)
+            halves = []
+            rights = []
             for r in range(envs):
                 high = parts[r].astype(jnp.bfloat16)
                 low = (parts[r] - high.astype(jnp.float32)).astype(jnp.bfloat16)
+                halves += [high, low]
                 rt = stack_ref[envs + r, s]
-                y = y + lax.dot_general(high, rt, nt, preferred_element_type=jnp.float32)
-                y = y + lax.dot_general(low, rt, nt, preferred_element_type=jnp.float32)
+                rights += [rt, rt]
+            y = jnp.dot(
+                jnp.concatenate(halves, axis=1),
+                jnp.concatenate(rights, axis=0),
+                preferred_element_type=jnp.float32,
+            )
             image[s] = y
             x = vec[s]
             return (sums[0] + _fold(x * x), sums[1] + _fold(x * y), sums[2] + _fold(y * y))
@@ -146,7 +156,7 @@
         scratch_shapes=[
             pltpu.VMEM((sectors, side, side), jnp.float32),
             pltpu.VMEM((sectors, side, side), jnp.float32),
-            pltpu.VMEM((sectors + 2 * HALO, side, side), jnp.bfloat16),
+            pltpu.VMEM((sectors + 2 * HALO, envs * side, envs * side), jnp.bfloat16),
         ],
         compiler_params=pltpu.CompilerParams(vmem_limit_bytes=48 * 1024 * 1024),
         cost_estimate=pl.CostEstimate(
@@ -170,7 +180,10 @@
         left_env, right_env = chain_envs(left_terms[0], left_rate[0], right_terms[0], right_rate[0])
     with jax.named_scope("env_gather"):
         stack = lax.all_gather(
-            jnp.concatenate([left_env, right_env, psi_start], axis=0), "sector", axis=1, tiled=True
+            jnp.concatenate([left_env, jnp.swapaxes(right_env, -1, -2), psi_start], axis=0),
+            "sector",
+            axis=1,
+            tiled=True,
         )
 
     envs = left_terms.shape[1]

time: 142 us -> 138 us (0.972)
  Pallas kernels: 38.1 us -> 34.1 us
    pallas_call x1, Pallas kernels: 38.1 us -> 34.1 us  [iterate(): pl.pallas_call(iterate_kernel, out_shape=(jax.ShapeDtypeStruct((local, si...]
where the time goes in v5:
time: 138 us
  waiting for transfers between devices  42.7 us (31%)
  Pallas kernels  34.1 us (25%)
  blocking collectives  20.1 us (15%)
  starting transfers between devices  17.2 us (12%)
  between operations  14.3 us (10%)
  local copies, waits for them, and re-layouts  5.55 us (4%)
  other arithmetic  3.27 us (2%)
    pallas_call x1, Pallas kernels, iterate(): pl.pallas_call(iterate_kernel, out_shape=(jax.ShapeDtypeStruct((local, si...  34.1 us
    all_gather x1, waiting for transfers between devices, body(): lax.all_gather(jnp.concatenate([left_env, jnp.swapaxes(right_env, -1, -2)...  26.4 us
    all_to_all x1, blocking collectives, chain_envs(): back = lax.all_to_all(env.astype(jnp.bfloat16), 'chain', 0, 0, tiled=True)  20.1 us
    all_to_all x1, starting transfers between devices, chain_envs(): spread = lax.all_to_all(packed, 'chain', 0, 0, tiled=True)  17.1 us
    all_to_all x1, waiting for transfers between devices, chain_envs(): spread = lax.all_to_all(packed, 'chain', 0, 0, tiled=True)  16.3 us
  transfers between devices with their start and end apart: 2, of which 2 were waited for; matrix products, arithmetic and copies ran while one was open for 0% of the time, Pallas kernels for 0%

profile of v5, /device:TPU:1, one launch (start us, length us, event | category | flops | bytes accessed | tf_op | source)
XLA Modules:
  0.0 137.6 jit_solution(1855505008744961711)
XLA Ops:
  7.2 0.8 stack.13
  7.9 0.1 copy.60
  8.0 0.8 stack.14
  8.8 0.1 copy.61
  8.9 0.1 pad.4
  9.0 0.3 copy.73
  9.2 1.8 %pad_maximum_fusion = bf16[64,32,128]{2,1,0:T(8,128)(2,1)} fusion(bf16[64,16,128]{2,1,0:T(8,128)(2,1)S(1)} %copy.73, bf16[64,8,128]{2,1,0:T(8,128)(2,1)} %bitcast.25, bf16[64,8,128]{2,1,0:T(8,128)(2,1)} %bitcast.26), kind=kLoop, calls=%fused_computation.2 | loop fusion | flops 1572864 | bytes 1048576 | tf_op jit(solution)/shard_map/env_chain/concatenate | solution.py:31
  11.1 17.1 %all-to-all-start = ((bf16[64,32,128]{2,1,0:T(8,128)(2,1)}), bf16[64,32,128]{2,1,0:T(8,128)(2,1)S(1)}, u32[]{:S(2)}, u32[]{:S(2)}) async-start(bf16[64,32,128]{2,1,0:T(8,128)(2,1)} %pad_maximum_fusion), calls=%async_computation | async-start | bytes 1048576 | tf_op jit(solution)/shard_map/env_chain/all_to_all | solution.py:35
  28.2 0.0 all-gather.2.cloned.1.call-start
  28.3 16.3 %all-to-all-done = bf16[64,32,128]{2,1,0:T(8,128)(2,1)S(1)} async-done(((bf16[64,32,128]{2,1,0:T(8,128)(2,1)}), bf16[64,32,128]{2,1,0:T(8,128)(2,1)S(1)}, u32[]{:S(2)}, u32[]{:S(2)}) %all-to-all-start) | async-done | bytes 524320 | tf_op jit(solution)/shard_map/env_chain/all_to_all | solution.py:35
  44.6 0.3 copy.74
  45.0 0.1 rev.6
  45.1 0.1 copy.68
  45.2 0.1 reduce_window_sum.18
  45.3 0.1 copy.69
  45.4 0.1 copy.65
  45.5 0.1 reduce_window_sum.17
  45.6 0.1 copy.66
  45.6 0.2 exponential_select_fusion
  45.9 0.4 fusion
  46.3 0.2 copy.71
  46.5 20.1 %all_to_all.10 = bf16[64,16,128]{2,1,0:T(8,128)(2,1)S(1)} all-to-all(bf16[64,16,128]{2,1,0:T(8,128)(2,1)S(1)} %copy.71), channel_id=1, replica_groups=mesh['chain'=64,'sector'=8] {'chain'}, dimensions={0} | all-to-all | bytes 524288 | tf_op jit(solution)/shard_map/env_chain/all_to_all | solution.py:58
  66.6 0.1 copy.72
  66.7 0.8 pad_maximum_fusion.1
  67.6 0.1 compare_convert_fusion
  67.7 0.1 multiply_reduce_fusion
  67.8 0.1 copy.59
  67.9 0.1 reshape.276.table_ref
  68.0 26.4 %all-gather.2.cloned.1.call-done.stack_ref = bf16[5,16,128,128]{3,2,1,0:T(8,128)(2,1)} async-done(((bf16[5,2,128,128]{3,2,1,0:T(8,128)(2,1)}), bf16[5,16,128,128]{3,2,1,0:T(8,128)(2,1)}) %all-gather.2.cloned.1.call-update) | async-done | bytes 2621456 | tf_op jit(solution)/shard_map/env_gather/all_gather | solution.py:182
  94.4 1.7 %copy-done = bf16[5,16,128,128]{3,2,1,0:T(8,128)(2,1)S(1)} copy-done((bf16[5,16,128,128]{3,2,1,0:T(8,128)(2,1)S(1)}, bf16[5,16,128,128]{3,2,1,0:T(8,128)(2,1)}, u32[]{:S(2)}) %copy-start) | copy-done | bytes 2621464
  96.1 34.1 %iterations.1 = (f32[2,128,128]{2,1,0:T(8,128)}, f32[8,128]{1,0:T(8,128)S(1)}) custom-call(f32[20]{0:T(128)S(1)} %reshape.276.table_ref, s32[1]{0:T(128)} %bitcast.place_ref, bf16[5,16,128,128]{3,2,1,0:T(8,128)(2,1)S(1)} %copy-done), custom_call_target="tpu_custom_call" | custom-call | flops 7516192768 | bytes 2752512 | tf_op jit(solution)/shard_map/iterations/pallas_call | solution.py:148
  130.2 0.5 slice.43
  (27 shorter events, 0.2 us)
Async XLA Ops:
  11.1 33.5 %all-to-all-start = ((bf16[64,32,128]{2,1,0:T(8,128)(2,1)}), bf16[64,32,128]{2,1,0:T(8,128)(2,1)S(1)}, u32[]{:S(2)}, u32[]{:S(2)}) async-start(bf16[64,32,128]{2,1,0:T(8,128)(2,1)} %pad_maximum_fusion), calls=%async_computation | async-start | bytes 1048576 | tf_op jit(solution)/shard_map/env_chain/all_to_all | solution.py:35
  28.2 66.1 %all-gather.2.cloned.1.call-start = ((), (), s32[]{:S(2)}) async-start(), calls=%async_computation.2 | async-start | bytes 2949120 | tf_op jit(solution)/shard_map/env_gather/all_gather | solution.py:182
  28.3 38.4 %copy-start.1 = (bf16[1,2,128,128]{3,2,1,0:T(8,128)(2,1)S(1)}, bf16[1,2,128,128]{3,2,1,0:T(8,128)(2,1)}, u32[]{:S(2)}) copy-start(bf16[1,2,128,128]{3,2,1,0:T(8,128)(2,1)} %param.9) | copy-start | bytes 196612
  44.9 22.6 %copy-start.5 = (s32[12]{0:T(128)S(1)}, s32[12]{0:T(128)}, u32[]{:S(2)}) copy-start(s32[12]{0:T(128)} %param.14) | copy-start | bytes 148
  45.0 22.6 %copy-start.3 = (f32[12]{0:T(128)S(1)}, f32[12]{0:T(128)}, u32[]{:S(2)}) copy-start(f32[12]{0:T(128)} %param.17) | copy-start | bytes 148
  45.0 22.6 %copy-start.4 = (s32[12]{0:T(128)S(1)}, s32[12]{0:T(128)}, u32[]{:S(2)}) copy-start(s32[12]{0:T(128)} %param.15) | copy-start | bytes 148
  45.0 22.6 %copy-start.2 = (s32[12]{0:T(128)S(1)}, s32[12]{0:T(128)}, u32[]{:S(2)}) copy-start(s32[12]{0:T(128)} %param.16) | copy-start | bytes 148
  94.4 1.7 %copy-start = (bf16[5,16,128,128]{3,2,1,0:T(8,128)(2,1)S(1)}, bf16[5,16,128,128]{3,2,1,0:T(8,128)(2,1)}, u32[]{:S(2)}) copy-start(bf16[5,16,128,128]{3,2,1,0:T(8,128)(2,1)} %all-gather.2.cloned.1.call-done.stack_ref) | copy-start | bytes 7864324
Sparse Core Ops, SparseCore 0:
  67.6 26.6 all-gather.1

commit v6 on v5

--- a/solution.py
+++ b/solution.py
@@ -18,25 +18,14 @@
     shape = left_terms.shape
     width = shape[-1]
     block = left_terms.size // width // count
-    rates = jnp.stack([left_rate.reshape(count, block), right_rate.reshape(count, block)], axis=1)
-    pieces = []
-    rest = rates
-    for _ in range(3):
-        piece = lax.reduce_precision(rest, exponent_bits=8, mantissa_bits=7)
-        rest = rest - piece
-        pieces.append(piece.astype(jnp.bfloat16))
-    coded = jnp.stack(pieces, axis=1).reshape(count, 6 * block)
-    coded = jnp.pad(coded, ((0, 0), (0, 2 * block * width - 6 * block)))
-    coded = coded.reshape(count, 2 * block, width)
     packed = jnp.concatenate(
-        [left_terms.reshape(count, block, width), right_terms.reshape(count, block, width), coded],
-        axis=1,
-    )
-    spread = lax.all_to_all(packed, "chain", 0, 0, tiled=True)
-    got = spread[:, 2 * block :].reshape(count, 2 * block * width)[:, : 6 * block]
-    got = got.astype(jnp.float32).reshape(count, 3, 2, block)
-    speed = (got[:, 0] + got[:, 1]) + got[:, 2]
-    spread = spread[:, : 2 * block].astype(jnp.float32)
+        [left_terms.reshape(count, block, width), right_terms.reshape(count, block, width)], axis=1
+    )
+    spread = lax.all_to_all(packed, "chain", 0, 0, tiled=True).astype(jnp.float32)
+    rates = jnp.stack([left_rate.reshape(1, count * block), right_rate.reshape(1, count * block)])
+    rates = lax.all_gather(rates, "chain", axis=1, tiled=True)
+    rates = rates.reshape(2, count, count, block)
+    speed = jnp.swapaxes(lax.dynamic_index_in_dim(rates, lax.axis_index("chain"), 2, False), 0, 1)
     ahead = jnp.cumsum(speed[:, 0], axis=0)
     behind = jnp.cumsum(speed[::-1, 1], axis=0)[::-1]
     order = jnp.arange(count)
@@ -76,10 +65,15 @@
     diag[...] = jnp.zeros(diag.shape, jnp.bfloat16)
     zero = jnp.zeros((8, side), jnp.float32)
     cosine = jnp.zeros((1, 1), jnp.float32)
+    scale = None
     for iteration in range(ITERS):
 
         def fill(s, carry):
-            w = vec[s].astype(jnp.bfloat16)
+            x = vec[s]
+            if scale is not None:
+                x = x * scale
+                vec[s] = x
+            w = x.astype(jnp.bfloat16)
             for e in range(envs):
                 diag[s + HALO, e * side : (e + 1) * side, e * side : (e + 1) * side] = w
             return carry
@@ -127,15 +121,9 @@
 
         su = _sum_all(lax.fori_loop(0, sectors, step, zero))
         scale = lax.rsqrt(su / entries + epsilon)
-
-        def norm(s, carry):
-            vec[s] = vec[s] * scale
-            return carry
-
-        lax.fori_loop(0, sectors, norm, 0)
         cosine = cross_dot * lax.rsqrt(self_dot * (image_dot + epsilon))
     local = out_ref.shape[0]
-    out_ref[...] = vec[pl.ds(place_ref[0] * local, local)]
+    out_ref[...] = vec[pl.ds(place_ref[0] * local, local)] * scale
     cos_ref[...] = jnp.broadcast_to(cosine, cos_ref.shape)
 
 

time: 138 us -> 171 us (1.24)
  blocking collectives: 20.1 us -> 60.9 us
  waiting for transfers between devices: 42.7 us -> 37.1 us
  local copies, waits for them, and re-layouts: 5.55 us -> 3.4 us
    all_gather x0 -> x1, blocking collectives: none -> 38.8 us  [chain_envs(): rates = lax.all_gather(rates, 'chain', axis=1, tiled=True)]
    all_to_all x1, waiting for transfers between devices: 16.3 us -> 0.01 us  [chain_envs(): lax.all_to_all(packed, 'chain', 0, 0, tiled=True).astype(jnp.float32)]
    all_gather x1, waiting for transfers between devices: 26.4 us -> 37.1 us  [body(): lax.all_gather(jnp.concatenate([left_env, jnp.swapaxes(right_env, -1, -2)...]
    all_to_all x1, blocking collectives: 20.1 us -> 22.1 us  [chain_envs(): back = lax.all_to_all(env.astype(jnp.bfloat16), 'chain', 0, 0, tiled=True)]
  transfers between devices with their start and end apart: 2 -> 2, of which waited for: 2 -> 1; matrix products, arithmetic and copies ran while one was open for 0% -> 1% of each run, Pallas kernels for 0% -> 0%
where the time goes in v6:
time: 171 us
  blocking collectives  60.9 us (36%)
  waiting for transfers between devices  37.1 us (22%)
  Pallas kernels  33.7 us (20%)
  starting transfers between devices  17.3 us (10%)
  between operations  14.2 us (8%)
  other arithmetic  3.81 us (2%)
  local copies, waits for them, and re-layouts  3.4 us (2%)
    all_gather x1, blocking collectives, chain_envs(): rates = lax.all_gather(rates, 'chain', axis=1, tiled=True)  38.8 us
    all_gather x1, waiting for transfers between devices, body(): lax.all_gather(jnp.concatenate([left_env, jnp.swapaxes(right_env, -1, -2)...  37.1 us
    pallas_call x1, Pallas kernels, iterate(): pl.pallas_call(iterate_kernel, out_shape=(jax.ShapeDtypeStruct((local, si...  33.7 us
    all_to_all x1, blocking collectives, chain_envs(): back = lax.all_to_all(env.astype(jnp.bfloat16), 'chain', 0, 0, tiled=True)  22.1 us
    all_to_all x1, starting transfers between devices, chain_envs(): lax.all_to_all(packed, 'chain', 0, 0, tiled=True).astype(jnp.float32)  17.3 us
  transfers between devices with their start and end apart: 2, of which 1 were waited for; matrix products, arithmetic and copies ran while one was open for 1% of the time, Pallas kernels for 0%

profile of v6, /device:TPU:1, one launch (start us, length us, event | category | flops | bytes accessed | tf_op | source)
XLA Modules:
  0.0 170.9 jit_solution(2759272745450448421)
XLA Ops:
  7.2 1.7 %pad_maximum_fusion.1 = bf16[64,16,128]{2,1,0:T(8,128)(2,1)} fusion(bf16[64,8,128]{2,1,0:T(8,128)(2,1)} %bitcast.24, bf16[64,8,128]{2,1,0:T(8,128)(2,1)} %bitcast.25), kind=kLoop, calls=%fused_computation.6 | loop fusion | flops 524288 | bytes 524288 | tf_op jit(solution)/shard_map/env_chain/concatenate | solution.py:21
  8.9 17.3 %all-to-all-start = ((bf16[64,16,128]{2,1,0:T(8,128)(2,1)}), bf16[64,16,128]{2,1,0:T(8,128)(2,1)S(1)}, u32[]{:S(2)}, u32[]{:S(2)}) async-start(bf16[64,16,128]{2,1,0:T(8,128)(2,1)} %pad_maximum_fusion.1), calls=%async_computation | async-start | bytes 524288 | tf_op jit(solution)/shard_map/env_chain/all_to_all | solution.py:24
  26.2 0.0 all-gather.2.cloned.1.call-start
  26.2 0.7 pad_maximum_fusion.2
  26.9 38.8 %all_gather.6 = f32[2,64,512]{2,0,1:T(2,128)S(1)} all-gather(f32[2,1,512]{2,0,1:T(2,128)S(1)} %copy.50), channel_id=1, replica_groups=mesh['chain'=64,'sector'=8] {'chain'}, dimensions={1}, use_global_device_ids=true | all-gather | bytes 266240 | tf_op jit(solution)/shard_map/env_chain/all_gather | solution.py:26
  65.7 0.2 copy.51
  66.0 0.0 copy-start.5
  66.0 0.0 copy-start.3
  66.0 0.0 copy-start.4
  66.0 0.0 copy-start.2
  66.0 0.1 rev.6
  66.1 0.1 copy.55
  66.2 0.1 reduce_window_sum.18
  66.3 0.1 copy.56
  66.4 0.1 copy.52
  66.5 0.1 reduce_window_sum.17
  66.6 0.1 copy.53
  66.7 0.2 exponential_select_fusion
  66.9 0.4 fusion
  67.3 0.2 copy.59
  67.5 22.1 %all_to_all.10 = bf16[64,16,128]{2,1,0:T(8,128)(2,1)S(1)} all-to-all(bf16[64,16,128]{2,1,0:T(8,128)(2,1)S(1)} %copy.59), channel_id=1, replica_groups=mesh['chain'=64,'sector'=8] {'chain'}, dimensions={0} | all-to-all | bytes 524288 | tf_op jit(solution)/shard_map/env_chain/all_to_all | solution.py:47
  89.6 0.1 copy.60
  89.8 0.8 pad_maximum_fusion
  90.6 0.0 all-gather.2.cloned.1.call-update
  90.7 0.1 compare_convert_fusion
  90.7 0.1 multiply_reduce_fusion
  90.8 0.1 copy.49
  90.9 0.1 reshape.142.table_ref
  91.0 37.1 %all-gather.2.cloned.1.call-done.stack_ref = bf16[5,16,128,128]{3,2,1,0:T(8,128)(2,1)} async-done(((bf16[5,2,128,128]{3,2,1,0:T(8,128)(2,1)}), bf16[5,16,128,128]{3,2,1,0:T(8,128)(2,1)}) %all-gather.2.cloned.1.call-update) | async-done | bytes 2621456 | tf_op jit(solution)/shard_map/env_gather/all_gather | solution.py:170
  128.1 1.7 %copy-done = bf16[5,16,128,128]{3,2,1,0:T(8,128)(2,1)S(1)} copy-done((bf16[5,16,128,128]{3,2,1,0:T(8,128)(2,1)S(1)}, bf16[5,16,128,128]{3,2,1,0:T(8,128)(2,1)}, u32[]{:S(2)}) %copy-start) | copy-done | bytes 2621464
  129.8 33.7 %iterations.1 = (f32[2,128,128]{2,1,0:T(8,128)}, f32[8,128]{1,0:T(8,128)S(1)}) custom-call(f32[20]{0:T(128)S(1)} %reshape.142.table_ref, s32[1]{0:T(128)} %bitcast.place_ref, bf16[5,16,128,128]{3,2,1,0:T(8,128)(2,1)S(1)} %copy-done), custom_call_target="tpu_custom_call" | custom-call | flops 7516192768 | bytes 2752512 | tf_op jit(solution)/shard_map/iterations/pallas_call | solution.py:136
  163.5 0.5 slice.19
  (19 shorter events, 0.1 us)
Async XLA Ops:
  8.9 80.9 %copy-start.1 = (bf16[1,2,128,128]{3,2,1,0:T(8,128)(2,1)S(1)}, bf16[1,2,128,128]{3,2,1,0:T(8,128)(2,1)}, u32[]{:S(2)}) copy-start(bf16[1,2,128,128]{3,2,1,0:T(8,128)(2,1)} %param.9) | copy-start | bytes 196612
  8.9 58.0 %all-to-all-start = ((bf16[64,16,128]{2,1,0:T(8,128)(2,1)}), bf16[64,16,128]{2,1,0:T(8,128)(2,1)S(1)}, u32[]{:S(2)}, u32[]{:S(2)}) async-start(bf16[64,16,128]{2,1,0:T(8,128)(2,1)} %pad_maximum_fusion.1), calls=%async_computation | async-start | bytes 524288 | tf_op jit(solution)/shard_map/env_chain/all_to_all | solution.py:24
  26.2 101.9 %all-gather.2.cloned.1.call-start = ((), (), s32[]{:S(2)}) async-start(), calls=%async_computation.2 | async-start | bytes 2949120 | tf_op jit(solution)/shard_map/env_gather/all_gather | solution.py:170
  66.0 24.6 %copy-start.5 = (s32[12]{0:T(128)S(1)}, s32[12]{0:T(128)}, u32[]{:S(2)}) copy-start(s32[12]{0:T(128)} %param.14) | copy-start | bytes 148
  66.0 24.6 %copy-start.3 = (f32[12]{0:T(128)S(1)}, f32[12]{0:T(128)}, u32[]{:S(2)}) copy-start(f32[12]{0:T(128)} %param.17) | copy-start | bytes 148
  66.0 24.6 %copy-start.4 = (s32[12]{0:T(128)S(1)}, s32[12]{0:T(128)}, u32[]{:S(2)}) copy-start(s32[12]{0:T(128)} %param.15) | copy-start | bytes 148
  66.0 24.7 %copy-start.2 = (s32[12]{0:T(128)S(1)}, s32[12]{0:T(128)}, u32[]{:S(2)}) copy-start(s32[12]{0:T(128)} %param.16) | copy-start | bytes 148
  128.1 1.7 %copy-start = (bf16[5,16,128,128]{3,2,1,0:T(8,128)(2,1)S(1)}, bf16[5,16,128,128]{3,2,1,0:T(8,128)(2,1)}, u32[]{:S(2)}) copy-start(bf16[5,16,128,128]{3,2,1,0:T(8,128)(2,1)} %all-gather.2.cloned.1.call-done.stack_ref) | copy-start | bytes 7864324
Sparse Core Ops, SparseCore 0:
  90.7 37.3 all-gather.1

commit v7 on v5

--- a/solution.py
+++ b/solution.py
@@ -76,15 +76,15 @@
     diag[...] = jnp.zeros(diag.shape, jnp.bfloat16)
     zero = jnp.zeros((8, side), jnp.float32)
     cosine = jnp.zeros((1, 1), jnp.float32)
+
+    def fill(s, carry):
+        w = vec[s].astype(jnp.bfloat16)
+        for e in range(envs):
+            diag[s + HALO, e * side : (e + 1) * side, e * side : (e + 1) * side] = w
+        return carry
+
+    lax.fori_loop(0, sectors, fill, 0)
     for iteration in range(ITERS):
-
-        def fill(s, carry):
-            w = vec[s].astype(jnp.bfloat16)
-            for e in range(envs):
-                diag[s + HALO, e * side : (e + 1) * side, e * side : (e + 1) * side] = w
-            return carry
-
-        lax.fori_loop(0, sectors, fill, 0)
 
         def apply(s, sums):
             lefts = jnp.concatenate([stack_ref[e, s] for e in range(envs)], axis=1)
@@ -119,20 +119,26 @@
         rayleigh_now = cross_dot / self_dot
         step_size = 0.5 * jnp.sqrt(self_dot / (image_dot + epsilon))
 
-        def step(s, su):
+        keep = 1.0 + step_size * rayleigh_now
+        update_sq = (
+            keep * keep * self_dot
+            - 2.0 * keep * step_size * cross_dot
+            + step_size * step_size * image_dot
+        )
+        scale = lax.rsqrt(update_sq / entries + epsilon)
+
+        def step(s, carry):
             x = vec[s]
             u = x - step_size * (image[s] - rayleigh_now * x)
-            vec[s] = u
-            return su + _fold(u * u)
-
-        su = _sum_all(lax.fori_loop(0, sectors, step, zero))
-        scale = lax.rsqrt(su / entries + epsilon)
-
-        def norm(s, carry):
-            vec[s] = vec[s] * scale
+            x = u * scale
+            vec[s] = x
+            if iteration + 1 < ITERS:
+                w = x.astype(jnp.bfloat16)
+                for e in range(envs):
+                    diag[s + HALO, e * side : (e + 1) * side, e * side : (e + 1) * side] = w
             return carry
 
-        lax.fori_loop(0, sectors, norm, 0)
+        lax.fori_loop(0, sectors, step, 0)
         cosine = cross_dot * lax.rsqrt(self_dot * (image_dot + epsilon))
     local = out_ref.shape[0]
     out_ref[...] = vec[pl.ds(place_ref[0] * local, local)]
@@ -160,7 +166,9 @@
         ],
         compiler_params=pltpu.CompilerParams(vmem_limit_bytes=48 * 1024 * 1024),
         cost_estimate=pl.CostEstimate(
-            flops=flops, transcendentals=0, bytes_accessed=stack.size * 2 + 4 * local * side * side
+            flops=flops,
+            transcendentals=0,
+            bytes_accessed=stack.size * 2 + 4 * local * side * side,
         ),
     )(table, place, stack)
 

time: 138 us -> 136 us (0.986)
  Pallas kernels: 34.1 us -> 32.6 us
    pallas_call x1, Pallas kernels: 34.1 us -> 32.6 us  [iterate(): pl.pallas_call(iterate_kernel, out_shape=(jax.ShapeDtypeStruct((local, si...]
where the time goes in v7:
time: 136 us
  waiting for transfers between devices  42.7 us (31%)
  Pallas kernels  32.6 us (24%)
  blocking collectives  20.1 us (15%)
  starting transfers between devices  17.2 us (13%)
  between operations  14.3 us (11%)
  local copies, waits for them, and re-layouts  5.55 us (4%)
  other arithmetic  3.27 us (2%)
    pallas_call x1, Pallas kernels, iterate(): pl.pallas_call(iterate_kernel, out_shape=(jax.ShapeDtypeStruct((local, si...  32.6 us
    all_gather x1, waiting for transfers between devices, body(): lax.all_gather(jnp.concatenate([left_env, jnp.swapaxes(right_env, -1, -2)...  26.4 us
    all_to_all x1, blocking collectives, chain_envs(): back = lax.all_to_all(env.astype(jnp.bfloat16), 'chain', 0, 0, tiled=True)  20.1 us
    all_to_all x1, starting transfers between devices, chain_envs(): spread = lax.all_to_all(packed, 'chain', 0, 0, tiled=True)  17.1 us
    all_to_all x1, waiting for transfers between devices, chain_envs(): spread = lax.all_to_all(packed, 'chain', 0, 0, tiled=True)  16.3 us
  transfers between devices with their start and end apart: 2, of which 2 were waited for; matrix products, arithmetic and copies ran while one was open for 0% of the time, Pallas kernels for 0%

profile of v7, /device:TPU:1, one launch (start us, length us, event | category | flops | bytes accessed | tf_op | source)
XLA Modules:
  0.0 136.1 jit_solution(9641541069276038445)
XLA Ops:
  7.2 0.8 stack.13
  7.9 0.1 copy.60
  8.0 0.8 stack.14
  8.8 0.1 copy.61
  8.9 0.1 pad.4
  9.0 0.3 copy.73
  9.2 1.8 %pad_maximum_fusion = bf16[64,32,128]{2,1,0:T(8,128)(2,1)} fusion(bf16[64,16,128]{2,1,0:T(8,128)(2,1)S(1)} %copy.73, bf16[64,8,128]{2,1,0:T(8,128)(2,1)} %bitcast.25, bf16[64,8,128]{2,1,0:T(8,128)(2,1)} %bitcast.26), kind=kLoop, calls=%fused_computation.2 | loop fusion | flops 1572864 | bytes 1048576 | tf_op jit(solution)/shard_map/env_chain/concatenate | solution.py:31
  11.1 17.1 %all-to-all-start = ((bf16[64,32,128]{2,1,0:T(8,128)(2,1)}), bf16[64,32,128]{2,1,0:T(8,128)(2,1)S(1)}, u32[]{:S(2)}, u32[]{:S(2)}) async-start(bf16[64,32,128]{2,1,0:T(8,128)(2,1)} %pad_maximum_fusion), calls=%async_computation | async-start | bytes 1048576 | tf_op jit(solution)/shard_map/env_chain/all_to_all | solution.py:35
  28.2 0.0 all-gather.2.cloned.1.call-start
  28.3 16.3 %all-to-all-done = bf16[64,32,128]{2,1,0:T(8,128)(2,1)S(1)} async-done(((bf16[64,32,128]{2,1,0:T(8,128)(2,1)}), bf16[64,32,128]{2,1,0:T(8,128)(2,1)S(1)}, u32[]{:S(2)}, u32[]{:S(2)}) %all-to-all-start) | async-done | bytes 524320 | tf_op jit(solution)/shard_map/env_chain/all_to_all | solution.py:35
  44.6 0.3 copy.74
  45.0 0.1 rev.6
  45.1 0.1 copy.68
  45.2 0.1 reduce_window_sum.18
  45.3 0.1 copy.69
  45.4 0.1 copy.65
  45.5 0.1 reduce_window_sum.17
  45.6 0.1 copy.66
  45.6 0.2 exponential_select_fusion
  45.9 0.4 fusion
  46.3 0.2 copy.71
  46.5 20.1 %all_to_all.10 = bf16[64,16,128]{2,1,0:T(8,128)(2,1)S(1)} all-to-all(bf16[64,16,128]{2,1,0:T(8,128)(2,1)S(1)} %copy.71), channel_id=1, replica_groups=mesh['chain'=64,'sector'=8] {'chain'}, dimensions={0} | all-to-all | bytes 524288 | tf_op jit(solution)/shard_map/env_chain/all_to_all | solution.py:58
  66.6 0.1 copy.72
  66.7 0.8 pad_maximum_fusion.1
  67.6 0.1 compare_convert_fusion
  67.7 0.1 multiply_reduce_fusion
  67.8 0.1 copy.59
  67.9 0.1 reshape.276.table_ref
  68.0 26.4 %all-gather.2.cloned.1.call-done.stack_ref = bf16[5,16,128,128]{3,2,1,0:T(8,128)(2,1)} async-done(((bf16[5,2,128,128]{3,2,1,0:T(8,128)(2,1)}), bf16[5,16,128,128]{3,2,1,0:T(8,128)(2,1)}) %all-gather.2.cloned.1.call-update) | async-done | bytes 2621456 | tf_op jit(solution)/shard_map/env_gather/all_gather | solution.py:190
  94.4 1.7 %copy-done = bf16[5,16,128,128]{3,2,1,0:T(8,128)(2,1)S(1)} copy-done((bf16[5,16,128,128]{3,2,1,0:T(8,128)(2,1)S(1)}, bf16[5,16,128,128]{3,2,1,0:T(8,128)(2,1)}, u32[]{:S(2)}) %copy-start) | copy-done | bytes 2621464
  96.1 32.6 %iterations.1 = (f32[2,128,128]{2,1,0:T(8,128)}, f32[8,128]{1,0:T(8,128)S(1)}) custom-call(f32[20]{0:T(128)S(1)} %reshape.276.table_ref, s32[1]{0:T(128)} %bitcast.place_ref, bf16[5,16,128,128]{3,2,1,0:T(8,128)(2,1)S(1)} %copy-done), custom_call_target="tpu_custom_call" | custom-call | flops 7516192768 | bytes 2752512 | tf_op jit(solution)/shard_map/iterations/pallas_call | solution.py:154
  128.7 0.5 slice.43
  (27 shorter events, 0.2 us)
Async XLA Ops:
  11.1 33.5 %all-to-all-start = ((bf16[64,32,128]{2,1,0:T(8,128)(2,1)}), bf16[64,32,128]{2,1,0:T(8,128)(2,1)S(1)}, u32[]{:S(2)}, u32[]{:S(2)}) async-start(bf16[64,32,128]{2,1,0:T(8,128)(2,1)} %pad_maximum_fusion), calls=%async_computation | async-start | bytes 1048576 | tf_op jit(solution)/shard_map/env_chain/all_to_all | solution.py:35
  28.2 66.1 %all-gather.2.cloned.1.call-start = ((), (), s32[]{:S(2)}) async-start(), calls=%async_computation.2 | async-start | bytes 2949120 | tf_op jit(solution)/shard_map/env_gather/all_gather | solution.py:190
  28.3 38.4 %copy-start.1 = (bf16[1,2,128,128]{3,2,1,0:T(8,128)(2,1)S(1)}, bf16[1,2,128,128]{3,2,1,0:T(8,128)(2,1)}, u32[]{:S(2)}) copy-start(bf16[1,2,128,128]{3,2,1,0:T(8,128)(2,1)} %param.9) | copy-start | bytes 196612
  44.9 22.6 %copy-start.5 = (s32[12]{0:T(128)S(1)}, s32[12]{0:T(128)}, u32[]{:S(2)}) copy-start(s32[12]{0:T(128)} %param.14) | copy-start | bytes 148
  45.0 22.6 %copy-start.3 = (f32[12]{0:T(128)S(1)}, f32[12]{0:T(128)}, u32[]{:S(2)}) copy-start(f32[12]{0:T(128)} %param.17) | copy-start | bytes 148
  45.0 22.6 %copy-start.4 = (s32[12]{0:T(128)S(1)}, s32[12]{0:T(128)}, u32[]{:S(2)}) copy-start(s32[12]{0:T(128)} %param.15) | copy-start | bytes 148
  45.0 22.6 %copy-start.2 = (s32[12]{0:T(128)S(1)}, s32[12]{0:T(128)}, u32[]{:S(2)}) copy-start(s32[12]{0:T(128)} %param.16) | copy-start | bytes 148
  94.4 1.7 %copy-start = (bf16[5,16,128,128]{3,2,1,0:T(8,128)(2,1)S(1)}, bf16[5,16,128,128]{3,2,1,0:T(8,128)(2,1)}, u32[]{:S(2)}) copy-start(bf16[5,16,128,128]{3,2,1,0:T(8,128)(2,1)} %all-gather.2.cloned.1.call-done.stack_ref) | copy-start | bytes 7864324
Sparse Core Ops, SparseCore 0:
  67.6 26.6 all-gather.1

commit v8 on v7

--- a/solution.py
+++ b/solution.py
@@ -114,7 +114,7 @@
             x = vec[s]
             return (sums[0] + _fold(x * x), sums[1] + _fold(x * y), sums[2] + _fold(y * y))
 
-        sx, sxy, sy = lax.fori_loop(0, sectors, apply, (zero, zero, zero))
+        sx, sxy, sy = lax.fori_loop(0, sectors, apply, (zero, zero, zero), unroll=16)
         self_dot, cross_dot, image_dot = _sum_all(sx), _sum_all(sxy), _sum_all(sy)
         rayleigh_now = cross_dot / self_dot
         step_size = 0.5 * jnp.sqrt(self_dot / (image_dot + epsilon))
@@ -138,7 +138,7 @@
                     diag[s + HALO, e * side : (e + 1) * side, e * side : (e + 1) * side] = w
             return carry
 
-        lax.fori_loop(0, sectors, step, 0)
+        lax.fori_loop(0, sectors, step, 0, unroll=4)
         cosine = cross_dot * lax.rsqrt(self_dot * (image_dot + epsilon))
     local = out_ref.shape[0]
     out_ref[...] = vec[pl.ds(place_ref[0] * local, local)]

time: 136 us -> 126 us (0.926)
  Pallas kernels: 32.6 us -> 22 us
    pallas_call x1, Pallas kernels: 32.6 us -> 22 us  [iterate(): pl.pallas_call(iterate_kernel, out_shape=(jax.ShapeDtypeStruct((local, si...]
where the time goes in v8:
time: 126 us; the launch traced here: 125 us
  waiting for transfers between devices  42.7 us (34%)
  Pallas kernels  22 us (17%)
  blocking collectives  20.1 us (16%)
  starting transfers between devices  17.2 us (14%)
  between operations  14.3 us (11%)
  local copies, waits for them, and re-layouts  5.55 us (4%)
  other arithmetic  3.27 us (3%)
    all_gather x1, waiting for transfers between devices, body(): lax.all_gather(jnp.concatenate([left_env, jnp.swapaxes(right_env, -1, -2)...  26.4 us
    pallas_call x1, Pallas kernels, iterate(): pl.pallas_call(iterate_kernel, out_shape=(jax.ShapeDtypeStruct((local, si...  22 us
    all_to_all x1, blocking collectives, chain_envs(): back = lax.all_to_all(env.astype(jnp.bfloat16), 'chain', 0, 0, tiled=True)  20.1 us
    all_to_all x1, starting transfers between devices, chain_envs(): spread = lax.all_to_all(packed, 'chain', 0, 0, tiled=True)  17.1 us
    all_to_all x1, waiting for transfers between devices, chain_envs(): spread = lax.all_to_all(packed, 'chain', 0, 0, tiled=True)  16.3 us
  transfers between devices with their start and end apart: 2, of which 2 were waited for; matrix products, arithmetic and copies ran while one was open for 0% of the time, Pallas kernels for 0%

profile of v8, /device:TPU:1, one launch (start us, length us, event | category | flops | bytes accessed | tf_op | source)
XLA Modules:
  0.0 125.4 jit_solution(4435990950611855285)
XLA Ops:
  7.2 0.8 stack.13
  7.9 0.1 copy.60
  8.0 0.8 stack.14
  8.8 0.1 copy.61
  8.9 0.1 pad.4
  9.0 0.3 copy.73
  9.2 1.8 %pad_maximum_fusion = bf16[64,32,128]{2,1,0:T(8,128)(2,1)} fusion(bf16[64,16,128]{2,1,0:T(8,128)(2,1)S(1)} %copy.73, bf16[64,8,128]{2,1,0:T(8,128)(2,1)} %bitcast.25, bf16[64,8,128]{2,1,0:T(8,128)(2,1)} %bitcast.26), kind=kLoop, calls=%fused_computation.2 | loop fusion | flops 1572864 | bytes 1048576 | tf_op jit(solution)/shard_map/env_chain/concatenate | solution.py:31
  11.1 17.1 %all-to-all-start = ((bf16[64,32,128]{2,1,0:T(8,128)(2,1)}), bf16[64,32,128]{2,1,0:T(8,128)(2,1)S(1)}, u32[]{:S(2)}, u32[]{:S(2)}) async-start(bf16[64,32,128]{2,1,0:T(8,128)(2,1)} %pad_maximum_fusion), calls=%async_computation | async-start | bytes 1048576 | tf_op jit(solution)/shard_map/env_chain/all_to_all | solution.py:35
  28.2 0.0 all-gather.2.cloned.1.call-start
  28.3 16.3 %all-to-all-done = bf16[64,32,128]{2,1,0:T(8,128)(2,1)S(1)} async-done(((bf16[64,32,128]{2,1,0:T(8,128)(2,1)}), bf16[64,32,128]{2,1,0:T(8,128)(2,1)S(1)}, u32[]{:S(2)}, u32[]{:S(2)}) %all-to-all-start) | async-done | bytes 524320 | tf_op jit(solution)/shard_map/env_chain/all_to_all | solution.py:35
  44.6 0.3 copy.74
  45.0 0.1 rev.6
  45.1 0.1 copy.68
  45.2 0.1 reduce_window_sum.18
  45.3 0.1 copy.69
  45.4 0.1 copy.65
  45.5 0.1 reduce_window_sum.17
  45.6 0.1 copy.66
  45.6 0.2 exponential_select_fusion
  45.9 0.4 fusion
  46.3 0.2 copy.71
  46.5 20.1 %all_to_all.10 = bf16[64,16,128]{2,1,0:T(8,128)(2,1)S(1)} all-to-all(bf16[64,16,128]{2,1,0:T(8,128)(2,1)S(1)} %copy.71), channel_id=1, replica_groups=mesh['chain'=64,'sector'=8] {'chain'}, dimensions={0} | all-to-all | bytes 524288 | tf_op jit(solution)/shard_map/env_chain/all_to_all | solution.py:58
  66.6 0.1 copy.72
  66.7 0.8 pad_maximum_fusion.1
  67.6 0.1 compare_convert_fusion
  67.7 0.1 multiply_reduce_fusion
  67.8 0.1 copy.59
  67.9 0.1 reshape.276.table_ref
  68.0 26.4 %all-gather.2.cloned.1.call-done.stack_ref = bf16[5,16,128,128]{3,2,1,0:T(8,128)(2,1)} async-done(((bf16[5,2,128,128]{3,2,1,0:T(8,128)(2,1)}), bf16[5,16,128,128]{3,2,1,0:T(8,128)(2,1)}) %all-gather.2.cloned.1.call-update) | async-done | bytes 2621456 | tf_op jit(solution)/shard_map/env_gather/all_gather | solution.py:190
  94.3 1.7 %copy-done = bf16[5,16,128,128]{3,2,1,0:T(8,128)(2,1)S(1)} copy-done((bf16[5,16,128,128]{3,2,1,0:T(8,128)(2,1)S(1)}, bf16[5,16,128,128]{3,2,1,0:T(8,128)(2,1)}, u32[]{:S(2)}) %copy-start) | copy-done | bytes 2621464
  96.1 22.0 %iterations.1 = (f32[2,128,128]{2,1,0:T(8,128)}, f32[8,128]{1,0:T(8,128)S(1)}) custom-call(f32[20]{0:T(128)S(1)} %reshape.276.table_ref, s32[1]{0:T(128)} %bitcast.place_ref, bf16[5,16,128,128]{3,2,1,0:T(8,128)(2,1)S(1)} %copy-done), custom_call_target="tpu_custom_call" | custom-call | flops 7516192768 | bytes 2752512 | tf_op jit(solution)/shard_map/iterations/pallas_call | solution.py:154
  118.1 0.5 slice.43
  (27 shorter events, 0.2 us)
Async XLA Ops:
  11.1 33.5 %all-to-all-start = ((bf16[64,32,128]{2,1,0:T(8,128)(2,1)}), bf16[64,32,128]{2,1,0:T(8,128)(2,1)S(1)}, u32[]{:S(2)}, u32[]{:S(2)}) async-start(bf16[64,32,128]{2,1,0:T(8,128)(2,1)} %pad_maximum_fusion), calls=%async_computation | async-start | bytes 1048576 | tf_op jit(solution)/shard_map/env_chain/all_to_all | solution.py:35
  28.2 66.1 %all-gather.2.cloned.1.call-start = ((), (), s32[]{:S(2)}) async-start(), calls=%async_computation.2 | async-start | bytes 2949120 | tf_op jit(solution)/shard_map/env_gather/all_gather | solution.py:190
  28.3 38.4 %copy-start.1 = (bf16[1,2,128,128]{3,2,1,0:T(8,128)(2,1)S(1)}, bf16[1,2,128,128]{3,2,1,0:T(8,128)(2,1)}, u32[]{:S(2)}) copy-start(bf16[1,2,128,128]{3,2,1,0:T(8,128)(2,1)} %param.9) | copy-start | bytes 196612
  44.9 22.6 %copy-start.5 = (s32[12]{0:T(128)S(1)}, s32[12]{0:T(128)}, u32[]{:S(2)}) copy-start(s32[12]{0:T(128)} %param.14) | copy-start | bytes 148
  45.0 22.6 %copy-start.3 = (f32[12]{0:T(128)S(1)}, f32[12]{0:T(128)}, u32[]{:S(2)}) copy-start(f32[12]{0:T(128)} %param.17) | copy-start | bytes 148
  45.0 22.6 %copy-start.4 = (s32[12]{0:T(128)S(1)}, s32[12]{0:T(128)}, u32[]{:S(2)}) copy-start(s32[12]{0:T(128)} %param.15) | copy-start | bytes 148
  45.0 22.6 %copy-start.2 = (s32[12]{0:T(128)S(1)}, s32[12]{0:T(128)}, u32[]{:S(2)}) copy-start(s32[12]{0:T(128)} %param.16) | copy-start | bytes 148
  94.3 1.7 %copy-start = (bf16[5,16,128,128]{3,2,1,0:T(8,128)(2,1)S(1)}, bf16[5,16,128,128]{3,2,1,0:T(8,128)(2,1)}, u32[]{:S(2)}) copy-start(bf16[5,16,128,128]{3,2,1,0:T(8,128)(2,1)} %all-gather.2.cloned.1.call-done.stack_ref) | copy-start | bytes 7864324
Sparse Core Ops, SparseCore 0:
  67.6 26.6 all-gather.1

commit v9 on v8

--- a/solution.py
+++ b/solution.py
@@ -67,12 +67,12 @@
     return jnp.sum(a.reshape(a.shape[0] // 8, 8, a.shape[1]), axis=0)
 
 
-def iterate_kernel(table_ref, place_ref, stack_ref, out_ref, cos_ref, vec, image, diag):
+def iterate_kernel(table_ref, place_ref, psi_ref, stack_ref, out_ref, cos_ref, vec, image, diag):
     _, sectors, side, _ = stack_ref.shape
-    envs = (stack_ref.shape[0] - 1) // 2
+    envs = stack_ref.shape[0] // 2
     shifts = 2 * HALO + 1
     entries = float(sectors * side * side)
-    vec[...] = stack_ref[2 * envs].astype(jnp.float32)
+    vec[...] = psi_ref[...]
     diag[...] = jnp.zeros(diag.shape, jnp.bfloat16)
     zero = jnp.zeros((8, side), jnp.float32)
     cosine = jnp.zeros((1, 1), jnp.float32)
@@ -145,11 +145,11 @@
     cos_ref[...] = jnp.broadcast_to(cosine, cos_ref.shape)
 
 
-def iterate(table, place, stack, local):
+def iterate(table, place, psi, stack, local):
     _, sectors, side, _ = stack.shape
     smem = pl.BlockSpec(memory_space=pltpu.SMEM)
     vmem = pl.BlockSpec(memory_space=pltpu.VMEM)
-    envs = (stack.shape[0] - 1) // 2
+    envs = stack.shape[0] // 2
     flops = ITERS * sectors * (2 * envs * (2 * HALO + 1) + 4 * envs) * 2 * side**3
     return pl.pallas_call(
         iterate_kernel,
@@ -157,7 +157,7 @@
             jax.ShapeDtypeStruct((local, side, side), jnp.float32),
             jax.ShapeDtypeStruct((8, 128), jnp.float32),
         ),
-        in_specs=[smem, smem, vmem],
+        in_specs=[smem, smem, vmem, vmem],
         out_specs=(vmem, vmem),
         scratch_shapes=[
             pltpu.VMEM((sectors, side, side), jnp.float32),
@@ -170,7 +170,7 @@
             transcendentals=0,
             bytes_accessed=stack.size * 2 + 4 * local * side * side,
         ),
-    )(table, place, stack)
+    )(table, place, psi, stack)
 
 
 def body(
@@ -184,11 +184,14 @@
     term_shift,
     term_coef,
 ):
+    with jax.named_scope("psi_gather"):
+        pair = jnp.concatenate([psi_start, psi_start], axis=0)
+        psi = lax.all_gather(pair, "sector", axis=1, tiled=True)[0].astype(jnp.float32)
     with jax.named_scope("env_chain"):
         left_env, right_env = chain_envs(left_terms[0], left_rate[0], right_terms[0], right_rate[0])
     with jax.named_scope("env_gather"):
         stack = lax.all_gather(
-            jnp.concatenate([left_env, jnp.swapaxes(right_env, -1, -2), psi_start], axis=0),
+            jnp.concatenate([left_env, jnp.swapaxes(right_env, -1, -2)], axis=0),
             "sector",
             axis=1,
             tiled=True,
@@ -209,7 +212,7 @@
     local = psi_start.shape[1]
     place = jnp.reshape(lax.axis_index("sector"), (1,)).astype(jnp.int32)
     with jax.named_scope("iterations"):
-        mine, cos = iterate(table, place, stack, local)
+        mine, cos = iterate(table, place, psi, stack, local)
     return (mine[None], jnp.reshape(cos[0, 0], (1,)))
 
 

time: 126 us -> 126 us (level)
  other arithmetic: 3.27 us -> 5.01 us
  waiting for transfers between devices: 42.7 us -> 41 us
  transfers between devices with their start and end apart: 2 -> 3, of which waited for: 2 -> 2; matrix products, arithmetic and copies ran while one was open for 0% -> 4% of each run, Pallas kernels for 0% -> 0%
where the time goes in v9:
time: 126 us; the launch traced here: 125 us
  waiting for transfers between devices  41 us (33%)
  Pallas kernels  21.8 us (17%)
  blocking collectives  20.1 us (16%)
  starting transfers between devices  17.2 us (14%)
  between operations  14.3 us (11%)
  local copies, waits for them, and re-layouts  5.42 us (4%)
  other arithmetic  5.01 us (4%)
    all_gather x1, waiting for transfers between devices, body(): lax.all_gather(jnp.concatenate([left_env, jnp.swapaxes(right_env, -1, -2)...  25.5 us
    pallas_call x1, Pallas kernels, iterate(): pl.pallas_call(iterate_kernel, out_shape=(jax.ShapeDtypeStruct((local, si...  21.8 us
    all_to_all x1, blocking collectives, chain_envs(): back = lax.all_to_all(env.astype(jnp.bfloat16), 'chain', 0, 0, tiled=True)  20.1 us
    all_to_all x1, starting transfers between devices, chain_envs(): spread = lax.all_to_all(packed, 'chain', 0, 0, tiled=True)  17.1 us
    all_to_all x1, waiting for transfers between devices, chain_envs(): spread = lax.all_to_all(packed, 'chain', 0, 0, tiled=True)  15.5 us
  transfers between devices with their start and end apart: 3, of which 2 were waited for; matrix products, arithmetic and copies ran while one was open for 4% of the time, Pallas kernels for 0%

profile of v9, /device:TPU:1, one launch (start us, length us, event | category | flops | bytes accessed | tf_op | source)
XLA Modules:
  0.0 125.3 jit_solution(12206587079989242992)
XLA Ops:
  7.2 0.8 stack.13
  8.0 0.8 stack.14
  8.8 0.1 copy.61
  8.9 0.1 pad.4
  9.0 0.3 copy.73
  9.3 1.8 %pad_maximum_fusion = bf16[64,32,128]{2,1,0:T(8,128)(2,1)} fusion(bf16[64,16,128]{2,1,0:T(8,128)(2,1)S(1)} %copy.73, bf16[64,8,128]{2,1,0:T(8,128)(2,1)} %bitcast.30, bf16[64,8,128]{2,1,0:T(8,128)(2,1)} %bitcast.31), kind=kLoop, calls=%fused_computation.4 | loop fusion | flops 1572864 | bytes 1048576 | tf_op jit(solution)/shard_map/env_chain/concatenate | solution.py:31
  11.1 17.1 %all-to-all-start = ((bf16[64,32,128]{2,1,0:T(8,128)(2,1)}), bf16[64,32,128]{2,1,0:T(8,128)(2,1)S(1)}, u32[]{:S(2)}, u32[]{:S(2)}) async-start(bf16[64,32,128]{2,1,0:T(8,128)(2,1)} %pad_maximum_fusion), calls=%async_computation | async-start | bytes 1048576 | tf_op jit(solution)/shard_map/env_chain/all_to_all | solution.py:35
  28.3 0.7 pad_maximum_fusion.2
  29.1 15.5 %all-to-all-done = bf16[64,32,128]{2,1,0:T(8,128)(2,1)S(1)} async-done(((bf16[64,32,128]{2,1,0:T(8,128)(2,1)}), bf16[64,32,128]{2,1,0:T(8,128)(2,1)S(1)}, u32[]{:S(2)}, u32[]{:S(2)}) %all-to-all-start) | async-done | bytes 524320 | tf_op jit(solution)/shard_map/env_chain/all_to_all | solution.py:35
  44.6 0.3 copy.74
  45.0 0.1 rev.6
  45.1 0.1 copy.68
  45.2 0.1 reduce_window_sum.18
  45.3 0.1 copy.69
  45.3 0.1 copy.65
  45.4 0.1 reduce_window_sum.17
  45.5 0.1 copy.66
  45.6 0.2 exponential_select_fusion
  45.8 0.4 fusion
  46.3 0.2 copy.71
  46.5 20.1 %all_to_all.10 = bf16[64,16,128]{2,1,0:T(8,128)(2,1)S(1)} all-to-all(bf16[64,16,128]{2,1,0:T(8,128)(2,1)S(1)} %copy.71), channel_id=1, replica_groups=mesh['chain'=64,'sector'=8] {'chain'}, dimensions={0} | all-to-all | bytes 524288 | tf_op jit(solution)/shard_map/env_chain/all_to_all | solution.py:58
  66.6 0.1 copy.72
  66.7 0.7 pad_maximum_fusion.1
  67.5 0.1 compare_convert_fusion
  67.6 0.1 multiply_reduce_fusion
  67.7 0.1 copy.59
  67.8 0.1 reshape.278.table_ref
  67.9 1.1 fusion.1.psi_ref
  69.0 25.5 %all-gather.5.cloned.1.call-done.stack_ref = bf16[4,16,128,128]{3,2,1,0:T(8,128)(2,1)} async-done(((bf16[4,2,128,128]{3,2,1,0:T(8,128)(2,1)}), bf16[4,16,128,128]{3,2,1,0:T(8,128)(2,1)}) %all-gather.5.cloned.1.call-update) | async-done | bytes 2097168 | tf_op jit(solution)/shard_map/env_gather/all_gather | solution.py:193
  94.5 1.6 %copy-done = bf16[4,16,128,128]{3,2,1,0:T(8,128)(2,1)S(1)} copy-done((bf16[4,16,128,128]{3,2,1,0:T(8,128)(2,1)S(1)}, bf16[4,16,128,128]{3,2,1,0:T(8,128)(2,1)}, u32[]{:S(2)}) %copy-start) | copy-done | bytes 2097176
  96.1 21.8 %iterations.1 = (f32[2,128,128]{2,1,0:T(8,128)}, f32[8,128]{1,0:T(8,128)S(1)}) custom-call(f32[20]{0:T(128)S(1)} %reshape.278.table_ref, s32[1]{0:T(128)} %bitcast.place_ref, f32[16,128,128]{2,1,0:T(8,128)S(1)} %fusion.1.psi_ref, bf16[4,16,128,128]{3,2,1,0:T(8,128)(2,1)S(1)} %copy-done), custom_call_target="tpu_custom_call" | custom-call | flops 7516192768 | bytes 2228224 | tf_op jit(solution)/shard_map/iterations/pallas_call | solution.py:154
  117.9 0.5 slice.47
  (32 shorter events, 0.3 us)
Async XLA Ops:
  7.2 21.1 %copy-start.1 = (bf16[1,2,128,128]{3,2,1,0:T(8,128)(2,1)S(1)}, bf16[1,2,128,128]{3,2,1,0:T(8,128)(2,1)}, u32[]{:S(2)}) copy-start(bf16[1,2,128,128]{3,2,1,0:T(8,128)(2,1)} %param.9) | copy-start | bytes 196612
  11.1 33.5 %all-to-all-start = ((bf16[64,32,128]{2,1,0:T(8,128)(2,1)}), bf16[64,32,128]{2,1,0:T(8,128)(2,1)S(1)}, u32[]{:S(2)}, u32[]{:S(2)}) async-start(bf16[64,32,128]{2,1,0:T(8,128)(2,1)} %pad_maximum_fusion), calls=%async_computation | async-start | bytes 1048576 | tf_op jit(solution)/shard_map/env_chain/all_to_all | solution.py:35
  28.2 39.7 %all-gather.3.cloned.1.call-start = ((), (), s32[]{:S(2)}) async-start(), calls=%async_computation.2 | async-start | bytes 1179648 | tf_op jit(solution)/shard_map/psi_gather/all_gather | solution.py:189
  29.0 65.6 %all-gather.5.cloned.1.call-start = ((), (), s32[]{:S(2)}) async-start(), calls=%async_computation.3 | async-start | bytes 2359296 | tf_op jit(solution)/shard_map/env_gather/all_gather | solution.py:193
  45.6 21.9 %copy-start.5 = (s32[12]{0:T(128)S(1)}, s32[12]{0:T(128)}, u32[]{:S(2)}) copy-start(s32[12]{0:T(128)} %param.14) | copy-start | bytes 148
  45.6 21.9 %copy-start.3 = (f32[12]{0:T(128)S(1)}, f32[12]{0:T(128)}, u32[]{:S(2)}) copy-start(f32[12]{0:T(128)} %param.17) | copy-start | bytes 148
  45.6 21.9 %copy-start.4 = (s32[12]{0:T(128)S(1)}, s32[12]{0:T(128)}, u32[]{:S(2)}) copy-start(s32[12]{0:T(128)} %param.15) | copy-start | bytes 148
  45.6 21.9 %copy-start.2 = (s32[12]{0:T(128)S(1)}, s32[12]{0:T(128)}, u32[]{:S(2)}) copy-start(s32[12]{0:T(128)} %param.16) | copy-start | bytes 148
  94.5 1.6 %copy-start = (bf16[4,16,128,128]{3,2,1,0:T(8,128)(2,1)S(1)}, bf16[4,16,128,128]{3,2,1,0:T(8,128)(2,1)}, u32[]{:S(2)}) copy-start(bf16[4,16,128,128]{3,2,1,0:T(8,128)(2,1)} %all-gather.5.cloned.1.call-done.stack_ref) | copy-start | bytes 6291460
Sparse Core Ops, SparseCore 0:
  31.8 30.3 all-gather.2
  67.6 26.9 all-gather.4

commit v10 on v8

--- a/solution.py
+++ b/solution.py
@@ -18,14 +18,16 @@
     shape = left_terms.shape
     width = shape[-1]
     block = left_terms.size // width // count
-    rates = jnp.stack([left_rate.reshape(count, block), right_rate.reshape(count, block)], axis=1)
-    pieces = []
-    rest = rates
-    for _ in range(3):
-        piece = lax.reduce_precision(rest, exponent_bits=8, mantissa_bits=7)
-        rest = rest - piece
-        pieces.append(piece.astype(jnp.bfloat16))
-    coded = jnp.stack(pieces, axis=1).reshape(count, 6 * block)
+    side = jnp.arange(2)[None, None, :, None]
+    rates = jnp.where(
+        side == 0, left_rate.reshape(count, 1, 1, block), right_rate.reshape(count, 1, 1, block)
+    )
+    part = jnp.arange(3)[None, :, None, None]
+    high = lax.reduce_precision(rates, exponent_bits=8, mantissa_bits=7)
+    mid = lax.reduce_precision(rates - high, exponent_bits=8, mantissa_bits=7)
+    low = (rates - high) - mid
+    coded = jnp.where(part == 0, high, jnp.where(part == 1, mid, low)).astype(jnp.bfloat16)
+    coded = coded.reshape(count, 6 * block)
     coded = jnp.pad(coded, ((0, 0), (0, 2 * block * width - 6 * block)))
     coded = coded.reshape(count, 2 * block, width)
     packed = jnp.concatenate(

time: 126 us -> 126 us (level)
    broadcast_in_dim x0 -> x8, local copies, waits for them, and re-layouts: none -> 1.99 us  [the longest x4 1.66 us: chain_envs(): jnp.where(side == 0, left_rate.reshape(count, 1, 1, block), right_rate.re...]
    another operation x4 -> x0, local copies, waits for them, and re-layouts: 1.66 us -> none  [chain_envs(): jnp.stack([left_rate.reshape(count, block), right_rate.reshape(count, blo...]
where the time goes in v10:
time: 126 us
  waiting for transfers between devices  42.7 us (34%)
  Pallas kernels  22 us (17%)
  blocking collectives  20.1 us (16%)
  starting transfers between devices  17.2 us (14%)
  between operations  14.3 us (11%)
  local copies, waits for them, and re-layouts  5.88 us (5%)
  other arithmetic  3.44 us (3%)
    all_gather x1, waiting for transfers between devices, body(): lax.all_gather(jnp.concatenate([left_env, jnp.swapaxes(right_env, -1, -2)...  26.4 us
    pallas_call x1, Pallas kernels, iterate(): pl.pallas_call(iterate_kernel, out_shape=(jax.ShapeDtypeStruct((local, si...  22 us
    all_to_all x1, blocking collectives, chain_envs(): back = lax.all_to_all(env.astype(jnp.bfloat16), 'chain', 0, 0, tiled=True)  20.1 us
    all_to_all x1, starting transfers between devices, chain_envs(): spread = lax.all_to_all(packed, 'chain', 0, 0, tiled=True)  17.1 us
    all_to_all x1, waiting for transfers between devices, chain_envs(): spread = lax.all_to_all(packed, 'chain', 0, 0, tiled=True)  16.3 us
  transfers between devices with their start and end apart: 2, of which 2 were waited for; matrix products, arithmetic and copies ran while one was open for 0% of the time, Pallas kernels for 0%

profile of v10, /device:TPU:1, one launch (start us, length us, event | category | flops | bytes accessed | tf_op | source)
XLA Modules:
  0.0 125.9 jit_solution(7185829612144276594)
XLA Ops:
  7.2 0.8 broadcast_in_dim.141
  8.0 0.8 broadcast_in_dim.143
  8.9 0.1 broadcast_in_dim.137
  8.9 0.1 broadcast_in_dim.138
  9.0 0.1 broadcast_in_dim.147
  9.1 0.1 broadcast_in_dim.148
  9.2 0.1 select_reduce-precision_fusion
  9.3 0.1 fusion.6
  9.4 0.1 pad.4
  9.5 0.3 copy.74
  9.8 1.8 %pad_maximum_fusion = bf16[64,32,128]{2,1,0:T(8,128)(2,1)} fusion(bf16[64,16,128]{2,1,0:T(8,128)(2,1)S(1)} %copy.74, bf16[64,8,128]{2,1,0:T(8,128)(2,1)} %bitcast.34, bf16[64,8,128]{2,1,0:T(8,128)(2,1)} %bitcast.35), kind=kLoop, calls=%fused_computation.2 | loop fusion | flops 1572864 | bytes 1048576 | tf_op jit(solution)/shard_map/env_chain/concatenate | solution.py:33
  11.6 17.1 %all-to-all-start = ((bf16[64,32,128]{2,1,0:T(8,128)(2,1)}), bf16[64,32,128]{2,1,0:T(8,128)(2,1)S(1)}, u32[]{:S(2)}, u32[]{:S(2)}) async-start(bf16[64,32,128]{2,1,0:T(8,128)(2,1)} %pad_maximum_fusion), calls=%async_computation | async-start | bytes 1048576 | tf_op jit(solution)/shard_map/env_chain/all_to_all | solution.py:37
  28.8 16.3 %all-to-all-done = bf16[64,32,128]{2,1,0:T(8,128)(2,1)S(1)} async-done(((bf16[64,32,128]{2,1,0:T(8,128)(2,1)}), bf16[64,32,128]{2,1,0:T(8,128)(2,1)S(1)}, u32[]{:S(2)}, u32[]{:S(2)}) %all-to-all-start) | async-done | bytes 524320 | tf_op jit(solution)/shard_map/env_chain/all_to_all | solution.py:37
  45.1 0.3 copy.75
  45.6 0.1 rev.6
  45.6 0.1 copy.69
  45.7 0.1 reduce_window_sum.18
  45.9 0.1 copy.66
  46.0 0.1 reduce_window_sum.17
  46.1 0.2 exponential_select_fusion
  46.4 0.4 fusion
  46.8 0.2 copy.72
  47.0 20.1 %all_to_all.10 = bf16[64,16,128]{2,1,0:T(8,128)(2,1)S(1)} all-to-all(bf16[64,16,128]{2,1,0:T(8,128)(2,1)S(1)} %copy.72), channel_id=1, replica_groups=mesh['chain'=64,'sector'=8] {'chain'}, dimensions={0} | all-to-all | bytes 524288 | tf_op jit(solution)/shard_map/env_chain/all_to_all | solution.py:60
  67.1 0.1 copy.73
  67.2 0.8 pad_maximum_fusion.1
  68.2 0.1 multiply_reduce_fusion
  68.3 0.1 copy.60
  68.4 0.1 reshape.192.table_ref
  68.5 26.4 %all-gather.2.cloned.1.call-done.stack_ref = bf16[5,16,128,128]{3,2,1,0:T(8,128)(2,1)} async-done(((bf16[5,2,128,128]{3,2,1,0:T(8,128)(2,1)}), bf16[5,16,128,128]{3,2,1,0:T(8,128)(2,1)}) %all-gather.2.cloned.1.call-update) | async-done | bytes 2621456 | tf_op jit(solution)/shard_map/env_gather/all_gather | solution.py:192
  94.9 1.7 %copy-done = bf16[5,16,128,128]{3,2,1,0:T(8,128)(2,1)S(1)} copy-done((bf16[5,16,128,128]{3,2,1,0:T(8,128)(2,1)S(1)}, bf16[5,16,128,128]{3,2,1,0:T(8,128)(2,1)}, u32[]{:S(2)}) %copy-start) | copy-done | bytes 2621464
  96.6 22.0 %iterations.1 = (f32[2,128,128]{2,1,0:T(8,128)}, f32[8,128]{1,0:T(8,128)S(1)}) custom-call(f32[20]{0:T(128)S(1)} %reshape.192.table_ref, s32[1]{0:T(128)} %bitcast.place_ref, bf16[5,16,128,128]{3,2,1,0:T(8,128)(2,1)S(1)} %copy-done), custom_call_target="tpu_custom_call" | custom-call | flops 7516192768 | bytes 2752512 | tf_op jit(solution)/shard_map/iterations/pallas_call | solution.py:156
  118.6 0.5 slice.43
  (34 shorter events, 0.5 us)
Async XLA Ops:
  11.6 33.5 %all-to-all-start = ((bf16[64,32,128]{2,1,0:T(8,128)(2,1)}), bf16[64,32,128]{2,1,0:T(8,128)(2,1)S(1)}, u32[]{:S(2)}, u32[]{:S(2)}) async-start(bf16[64,32,128]{2,1,0:T(8,128)(2,1)} %pad_maximum_fusion), calls=%async_computation | async-start | bytes 1048576 | tf_op jit(solution)/shard_map/env_chain/all_to_all | solution.py:37
  28.7 66.1 %all-gather.2.cloned.1.call-start = ((), (), s32[]{:S(2)}) async-start(), calls=%async_computation.2 | async-start | bytes 2949120 | tf_op jit(solution)/shard_map/env_gather/all_gather | solution.py:192
  28.8 38.4 %copy-start.1 = (bf16[1,2,128,128]{3,2,1,0:T(8,128)(2,1)S(1)}, bf16[1,2,128,128]{3,2,1,0:T(8,128)(2,1)}, u32[]{:S(2)}) copy-start(bf16[1,2,128,128]{3,2,1,0:T(8,128)(2,1)} %param.9) | copy-start | bytes 196612
  45.5 22.6 %copy-start.5 = (s32[12]{0:T(128)S(1)}, s32[12]{0:T(128)}, u32[]{:S(2)}) copy-start(s32[12]{0:T(128)} %param.14) | copy-start | bytes 148
  45.5 22.6 %copy-start.3 = (f32[12]{0:T(128)S(1)}, f32[12]{0:T(128)}, u32[]{:S(2)}) copy-start(f32[12]{0:T(128)} %param.17) | copy-start | bytes 148
  45.5 22.6 %copy-start.4 = (s32[12]{0:T(128)S(1)}, s32[12]{0:T(128)}, u32[]{:S(2)}) copy-start(s32[12]{0:T(128)} %param.15) | copy-start | bytes 148
  45.5 22.6 %copy-start.2 = (s32[12]{0:T(128)S(1)}, s32[12]{0:T(128)}, u32[]{:S(2)}) copy-start(s32[12]{0:T(128)} %param.16) | copy-start | bytes 148
  94.9 1.7 %copy-start = (bf16[5,16,128,128]{3,2,1,0:T(8,128)(2,1)S(1)}, bf16[5,16,128,128]{3,2,1,0:T(8,128)(2,1)}, u32[]{:S(2)}) copy-start(bf16[5,16,128,128]{3,2,1,0:T(8,128)(2,1)} %all-gather.2.cloned.1.call-done.stack_ref) | copy-start | bytes 7864324
Sparse Core Ops, SparseCore 0:
  68.2 26.6 all-gather.1

commit v11 on v8

--- a/solution.py
+++ b/solution.py
@@ -73,7 +73,14 @@
     shifts = 2 * HALO + 1
     entries = float(sectors * side * side)
     vec[...] = stack_ref[2 * envs].astype(jnp.float32)
-    diag[...] = jnp.zeros(diag.shape, jnp.bfloat16)
+    block = jnp.zeros((diag.shape[0], side, side), jnp.bfloat16)
+    for e in range(envs):
+        for f in range(envs):
+            if e != f:
+                diag[:, e * side : (e + 1) * side, f * side : (f + 1) * side] = block
+    rim = jnp.zeros((HALO,) + diag.shape[1:], jnp.bfloat16)
+    diag[0:HALO] = rim
+    diag[HALO + sectors : 2 * HALO + sectors] = rim
     zero = jnp.zeros((8, side), jnp.float32)
     cosine = jnp.zeros((1, 1), jnp.float32)
 
@@ -83,7 +90,7 @@
             diag[s + HALO, e * side : (e + 1) * side, e * side : (e + 1) * side] = w
         return carry
 
-    lax.fori_loop(0, sectors, fill, 0)
+    lax.fori_loop(0, sectors, fill, 0, unroll=True)
     for iteration in range(ITERS):
 
         def apply(s, sums):
@@ -138,7 +145,7 @@
                     diag[s + HALO, e * side : (e + 1) * side, e * side : (e + 1) * side] = w
             return carry
 
-        lax.fori_loop(0, sectors, step, 0, unroll=4)
+        lax.fori_loop(0, sectors, step, 0, unroll=True)
         cosine = cross_dot * lax.rsqrt(self_dot * (image_dot + epsilon))
     local = out_ref.shape[0]
     out_ref[...] = vec[pl.ds(place_ref[0] * local, local)]

time: 126 us -> 126 us (level)
  no operation moved by 1% of the time
where the time goes in v11:
time: 126 us; the launch traced here: 125 us
  waiting for transfers between devices  42.7 us (34%)
  Pallas kernels  21.8 us (17%)
  blocking collectives  20.1 us (16%)
  starting transfers between devices  17.2 us (14%)
  between operations  14.3 us (11%)
  local copies, waits for them, and re-layouts  5.55 us (4%)
  other arithmetic  3.27 us (3%)
    all_gather x1, waiting for transfers between devices, body(): lax.all_gather(jnp.concatenate([left_env, jnp.swapaxes(right_env, -1, -2)...  26.4 us
    pallas_call x1, Pallas kernels, iterate(): pl.pallas_call(iterate_kernel, out_shape=(jax.ShapeDtypeStruct((local, si...  21.8 us
    all_to_all x1, blocking collectives, chain_envs(): back = lax.all_to_all(env.astype(jnp.bfloat16), 'chain', 0, 0, tiled=True)  20.1 us
    all_to_all x1, starting transfers between devices, chain_envs(): spread = lax.all_to_all(packed, 'chain', 0, 0, tiled=True)  17.1 us
    all_to_all x1, waiting for transfers between devices, chain_envs(): spread = lax.all_to_all(packed, 'chain', 0, 0, tiled=True)  16.3 us
  transfers between devices with their start and end apart: 2, of which 2 were waited for; matrix products, arithmetic and copies ran while one was open for 0% of the time, Pallas kernels for 0%

profile of v11, /device:TPU:1, one launch (start us, length us, event | category | flops | bytes accessed | tf_op | source)
XLA Modules:
  0.0 125.2 jit_solution(9863503920866502913)
XLA Ops:
  7.2 0.8 stack.13
  7.9 0.1 copy.60
  8.0 0.8 stack.14
  8.8 0.1 copy.61
  8.9 0.1 pad.4
  9.0 0.3 copy.73
  9.2 1.8 %pad_maximum_fusion = bf16[64,32,128]{2,1,0:T(8,128)(2,1)} fusion(bf16[64,16,128]{2,1,0:T(8,128)(2,1)S(1)} %copy.73, bf16[64,8,128]{2,1,0:T(8,128)(2,1)} %bitcast.25, bf16[64,8,128]{2,1,0:T(8,128)(2,1)} %bitcast.26), kind=kLoop, calls=%fused_computation.2 | loop fusion | flops 1572864 | bytes 1048576 | tf_op jit(solution)/shard_map/env_chain/concatenate | solution.py:31
  11.1 17.1 %all-to-all-start = ((bf16[64,32,128]{2,1,0:T(8,128)(2,1)}), bf16[64,32,128]{2,1,0:T(8,128)(2,1)S(1)}, u32[]{:S(2)}, u32[]{:S(2)}) async-start(bf16[64,32,128]{2,1,0:T(8,128)(2,1)} %pad_maximum_fusion), calls=%async_computation | async-start | bytes 1048576 | tf_op jit(solution)/shard_map/env_chain/all_to_all | solution.py:35
  28.2 0.0 all-gather.2.cloned.1.call-start
  28.3 16.3 %all-to-all-done = bf16[64,32,128]{2,1,0:T(8,128)(2,1)S(1)} async-done(((bf16[64,32,128]{2,1,0:T(8,128)(2,1)}), bf16[64,32,128]{2,1,0:T(8,128)(2,1)S(1)}, u32[]{:S(2)}, u32[]{:S(2)}) %all-to-all-start) | async-done | bytes 524320 | tf_op jit(solution)/shard_map/env_chain/all_to_all | solution.py:35
  44.6 0.3 copy.74
  45.0 0.1 rev.6
  45.1 0.1 copy.68
  45.2 0.1 reduce_window_sum.18
  45.3 0.1 copy.69
  45.4 0.1 copy.65
  45.5 0.1 reduce_window_sum.17
  45.6 0.1 copy.66
  45.6 0.2 exponential_select_fusion
  45.9 0.4 fusion
  46.3 0.2 copy.71
  46.5 20.1 %all_to_all.10 = bf16[64,16,128]{2,1,0:T(8,128)(2,1)S(1)} all-to-all(bf16[64,16,128]{2,1,0:T(8,128)(2,1)S(1)} %copy.71), channel_id=1, replica_groups=mesh['chain'=64,'sector'=8] {'chain'}, dimensions={0} | all-to-all | bytes 524288 | tf_op jit(solution)/shard_map/env_chain/all_to_all | solution.py:58
  66.6 0.1 copy.72
  66.7 0.8 pad_maximum_fusion.1
  67.6 0.1 compare_convert_fusion
  67.7 0.1 multiply_reduce_fusion
  67.8 0.1 copy.59
  67.9 0.1 reshape.276.table_ref
  68.0 26.4 %all-gather.2.cloned.1.call-done.stack_ref = bf16[5,16,128,128]{3,2,1,0:T(8,128)(2,1)} async-done(((bf16[5,2,128,128]{3,2,1,0:T(8,128)(2,1)}), bf16[5,16,128,128]{3,2,1,0:T(8,128)(2,1)}) %all-gather.2.cloned.1.call-update) | async-done | bytes 2621456 | tf_op jit(solution)/shard_map/env_gather/all_gather | solution.py:197
  94.4 1.7 %copy-done = bf16[5,16,128,128]{3,2,1,0:T(8,128)(2,1)S(1)} copy-done((bf16[5,16,128,128]{3,2,1,0:T(8,128)(2,1)S(1)}, bf16[5,16,128,128]{3,2,1,0:T(8,128)(2,1)}, u32[]{:S(2)}) %copy-start) | copy-done | bytes 2621464
  96.1 21.8 %iterations.1 = (f32[2,128,128]{2,1,0:T(8,128)}, f32[8,128]{1,0:T(8,128)S(1)}) custom-call(f32[20]{0:T(128)S(1)} %reshape.276.table_ref, s32[1]{0:T(128)} %bitcast.place_ref, bf16[5,16,128,128]{3,2,1,0:T(8,128)(2,1)S(1)} %copy-done), custom_call_target="tpu_custom_call" | custom-call | flops 7516192768 | bytes 2752512 | tf_op jit(solution)/shard_map/iterations/pallas_call | solution.py:161
  117.9 0.5 slice.43
  (27 shorter events, 0.2 us)
Async XLA Ops:
  11.1 33.5 %all-to-all-start = ((bf16[64,32,128]{2,1,0:T(8,128)(2,1)}), bf16[64,32,128]{2,1,0:T(8,128)(2,1)S(1)}, u32[]{:S(2)}, u32[]{:S(2)}) async-start(bf16[64,32,128]{2,1,0:T(8,128)(2,1)} %pad_maximum_fusion), calls=%async_computation | async-start | bytes 1048576 | tf_op jit(solution)/shard_map/env_chain/all_to_all | solution.py:35
  28.2 66.1 %all-gather.2.cloned.1.call-start = ((), (), s32[]{:S(2)}) async-start(), calls=%async_computation.2 | async-start | bytes 2949120 | tf_op jit(solution)/shard_map/env_gather/all_gather | solution.py:197
  28.3 38.4 %copy-start.1 = (bf16[1,2,128,128]{3,2,1,0:T(8,128)(2,1)S(1)}, bf16[1,2,128,128]{3,2,1,0:T(8,128)(2,1)}, u32[]{:S(2)}) copy-start(bf16[1,2,128,128]{3,2,1,0:T(8,128)(2,1)} %param.9) | copy-start | bytes 196612
  44.9 22.6 %copy-start.5 = (s32[12]{0:T(128)S(1)}, s32[12]{0:T(128)}, u32[]{:S(2)}) copy-start(s32[12]{0:T(128)} %param.14) | copy-start | bytes 148
  45.0 22.6 %copy-start.3 = (f32[12]{0:T(128)S(1)}, f32[12]{0:T(128)}, u32[]{:S(2)}) copy-start(f32[12]{0:T(128)} %param.17) | copy-start | bytes 148
  45.0 22.6 %copy-start.4 = (s32[12]{0:T(128)S(1)}, s32[12]{0:T(128)}, u32[]{:S(2)}) copy-start(s32[12]{0:T(128)} %param.15) | copy-start | bytes 148
  45.0 22.6 %copy-start.2 = (s32[12]{0:T(128)S(1)}, s32[12]{0:T(128)}, u32[]{:S(2)}) copy-start(s32[12]{0:T(128)} %param.16) | copy-start | bytes 148
  94.4 1.7 %copy-start = (bf16[5,16,128,128]{3,2,1,0:T(8,128)(2,1)S(1)}, bf16[5,16,128,128]{3,2,1,0:T(8,128)(2,1)}, u32[]{:S(2)}) copy-start(bf16[5,16,128,128]{3,2,1,0:T(8,128)(2,1)} %all-gather.2.cloned.1.call-done.stack_ref) | copy-start | bytes 7864324
Sparse Core Ops, SparseCore 0:
  67.6 26.6 all-gather.1
